TPU v7x, 512 devices: a whole 4x4x16 slice. The times are simulated.
512 devices in a mesh: seq: 128 (over x, z, y_hi), batch: 4 (over y_lo, core).
Axes of the slice: x: 4, y: 4 (y_hi: 2, y_lo: 2; y = y_hi * 2 + y_lo), z: 16, core: 2. Of those that a mesh axis runs over, the one named last changes fastest.
Arguments:
- inputs: bfloat16 [4, 128, 16384], P('batch', None, 'seq'), may hold values from -6 to 6
- out_grad: bfloat16 [4, 128, 16384], P('batch', None, 'seq'), may hold values from -0.046875 to 0.046875
- filters: float32 [128, 16384], P(None, 'seq'), may hold values from -6 to 6
Outputs:
- in_grad: bfloat16 [4, 128, 16384], P('batch', None, 'seq')
- filter_grad: float32 [128, 16384], P(None, 'seq')
All inputs are finite; a program needn't handle non-finite values.
Results may differ from a plain program's by a relative error of at most 0.0025.
Values sent between devices are 32-bit elements; how exact they have to be, the bound alone decides.
No kernel may reach another device: no remote copies, remote signals or barrier semaphores. Data moves between devices by JAX's collectives and lax.ppermute only.
A program may use at most 64 MiB of HBM per device.

v0:
```python
import math

import jax
import jax.numpy as jnp
from jax import lax
from jax.sharding import PartitionSpec as P

FACTOR = 16


def contract(pattern, operand, weights):
    return jnp.einsum(
        pattern,
        operand,
        weights,
        precision=lax.Precision.HIGHEST,
        preferred_element_type=jnp.float32,
    )


def angles(left_index, right_index, modulus):
    product = left_index[:, None] * right_index[None, :] % modulus
    return product.astype(jnp.float32) * (2.0 * math.pi / modulus)


def rotate(pattern, real_part, imag_part, angle_table, orient):
    cosine = jnp.cos(angle_table)
    sine_part = jnp.sin(angle_table)
    new_real = contract(pattern, real_part, cosine) - orient * contract(
        pattern, imag_part, sine_part
    )
    new_imag = contract(pattern, imag_part, cosine) + orient * contract(
        pattern, real_part, sine_part
    )
    return (new_real, new_imag)


def twist(real_part, imag_part, angle_table, orient):
    cosine = jnp.cos(angle_table)
    sine_part = jnp.sin(angle_table)
    return (
        real_part * cosine - orient * imag_part * sine_part,
        imag_part * cosine + orient * real_part * sine_part,
    )


def local_tables(length_all):
    inner = length_all // FACTOR
    outer_index = jnp.arange(FACTOR, dtype=jnp.int32)
    inner_index = jnp.arange(inner, dtype=jnp.int32)
    outer_table = angles(outer_index, outer_index, FACTOR)
    mid_table = angles(outer_index, inner_index, length_all)
    inner_table = angles(inner_index, inner_index, inner)
    return (outer_table, mid_table, inner_table)


def local_forward(real_part, imag_part):
    row_count, held, length_all = real_part.shape
    outer_table, mid_table, inner_table = local_tables(length_all)
    real_part = real_part.reshape(row_count, held, FACTOR, length_all // FACTOR)
    imag_part = imag_part.reshape(row_count, held, FACTOR, length_all // FACTOR)
    real_part, imag_part = rotate("kiuv,uq->kiqv", real_part, imag_part, outer_table, -1.0)
    real_part, imag_part = twist(real_part, imag_part, mid_table, -1.0)
    return rotate("kiqv,vm->kiqm", real_part, imag_part, inner_table, -1.0)


def local_inverse(real_part, imag_part):
    row_count, held, outer, inner = real_part.shape
    outer_table, mid_table, inner_table = local_tables(outer * inner)
    real_part, imag_part = rotate("kiqm,mv->kiqv", real_part, imag_part, inner_table, 1.0)
    real_part, imag_part = twist(real_part, imag_part, mid_table, 1.0)
    real_part, imag_part = rotate("kiqv,qu->kiuv", real_part, imag_part, outer_table, 1.0)
    return (
        real_part.reshape(row_count, held, outer * inner),
        imag_part.reshape(row_count, held, outer * inner),
    )


def body(inputs, out_grad, filters):
    seq_count = lax.axis_size("seq")
    position = lax.axis_index("seq")
    length_dev = inputs.shape[2]
    block_len = length_dev // seq_count
    total_len = 2 * seq_count * length_dev
    channels = inputs.shape[1]
    stacked = jnp.concatenate(
        [inputs[0].astype(jnp.float32), out_grad[0].astype(jnp.float32), filters], axis=0
    )
    row_count = stacked.shape[0]
    spread = lax.all_to_all(
        stacked.reshape(row_count, seq_count, block_len),
        "seq",
        split_axis=1,
        concat_axis=1,
        tiled=True,
    )
    low_index = jnp.arange(seq_count, dtype=jnp.int32)
    second_freq = jnp.where(low_index == 0, seq_count, 2 * seq_count - low_index)
    freq_order = jnp.stack([low_index, second_freq], axis=1).reshape(2 * seq_count)
    cross_table = angles(low_index, freq_order, 2 * seq_count)
    local_cols = position * block_len + jnp.arange(block_len, dtype=jnp.int32)
    cols_twist = angles(freq_order, local_cols, total_len)
    real_part = contract("kaj,am->kmj", spread, jnp.cos(cross_table))
    imag_part = -contract("kaj,am->kmj", spread, jnp.sin(cross_table))
    real_part, imag_part = twist(real_part, imag_part, cols_twist, -1.0)
    cols_real, cols_imag = (
        lax.all_to_all(real_part, "seq", split_axis=1, concat_axis=2, tiled=True),
        lax.all_to_all(imag_part, "seq", split_axis=1, concat_axis=2, tiled=True),
    )
    spec_real, spec_imag = local_forward(cols_real, cols_imag)
    input_real = spec_real[:channels]
    input_imag = spec_imag[:channels]
    grad_real = spec_real[channels : 2 * channels]
    grad_imag = spec_imag[channels : 2 * channels]
    filter_real = spec_real[2 * channels :]
    filter_imag = spec_imag[2 * channels :]
    first_real = filter_real * grad_real + filter_imag * grad_imag
    first_imag = filter_real * grad_imag - filter_imag * grad_real
    second_real = input_real * grad_real + input_imag * grad_imag
    second_imag = input_real * grad_imag - input_imag * grad_real
    joined_real = jnp.concatenate([first_real, second_real], axis=0)
    joined_imag = jnp.concatenate([first_imag, second_imag], axis=0)
    held_freq = lax.dynamic_slice_in_dim(freq_order, 2 * position, 2)
    all_cols = jnp.arange(length_dev, dtype=jnp.int32)
    back_twist = angles(held_freq, all_cols, total_len)
    back_table = angles(freq_order, low_index, 2 * seq_count)
    factor_scale = 1.0 / total_len
    cos_back = jnp.cos(back_table) * factor_scale
    sin_back = jnp.sin(back_table) * factor_scale
    back_real, back_imag = local_inverse(joined_real, joined_imag)
    back_real, back_imag = twist(back_real, back_imag, back_twist, 1.0)
    gath_real, gath_imag = (
        lax.all_to_all(back_real, "seq", split_axis=2, concat_axis=1, tiled=True),
        lax.all_to_all(back_imag, "seq", split_axis=2, concat_axis=1, tiled=True),
    )
    rebuilt = contract("kmj,ma->kaj", gath_real, cos_back) - contract(
        "kmj,ma->kaj", gath_imag, sin_back
    )
    returned = lax.all_to_all(rebuilt, "seq", split_axis=1, concat_axis=2, tiled=True)[:, 0, :]
    in_grad = returned[:channels].astype(jnp.bfloat16)[None]
    partial_grad = returned[channels:]
    filter_grad = lax.psum(partial_grad, "batch")
    return (in_grad, filter_grad)


def solution(mesh):
    placed = (P("batch", None, "seq"), P("batch", None, "seq"), P(None, "seq"))
    return jax.shard_map(
        body,
        mesh=mesh,
        in_specs=placed,
        out_specs=(P("batch", None, "seq"), P(None, "seq")),
        check_vma=False,
    )
```

profile of v0, /device:TPU:1, one launch (start us, length us, event | category | flops | bytes accessed | tf_op | source)
XLA Modules:
  0.0 269.2 jit_solution(8236200142034256242)
XLA Ops:
  7.2 0.0 copy-start.1
  7.2 0.0 copy-start
  7.2 0.9 copy.67
  8.1 0.0 copy-done.1
  8.1 0.1 copy.68
  8.2 0.0 copy-done
  8.2 0.1 copy.69
  8.4 0.8 reshape.208
  9.2 23.0 %all-to-all-start = ((f32[384,128,1]{0,2,1:T(1,128)}), f32[384,128,1]{0,2,1:T(1,128)S(1)}, u32[]{:S(2)}, u32[]{:S(2)}) async-start(f32[384,128,1]{0,2,1:T(1,128)} %reshape.208), calls=%async_computation | async-start | bytes 393216 | tf_op jit(solution)/shard_map/all_to_all | solution.py:90
  32.2 0.1 copy.66
  32.3 0.1 mul.547
  32.4 0.1 fusion.201
  32.5 19.3 %all-to-all-done = f32[384,128,1]{0,2,1:T(1,128)S(1)} async-done(((f32[384,128,1]{0,2,1:T(1,128)}), f32[384,128,1]{0,2,1:T(1,128)S(1)}, u32[]{:S(2)}, u32[]{:S(2)}) %all-to-all-start) | async-done | bytes 196640 | tf_op jit(solution)/shard_map/all_to_all | solution.py:90
  51.8 1.0 fusion
  52.8 1.0 add_bitcast_fusion.1
  53.8 1.2 copy.70
  55.0 7.5 %all-to-all-start.1 = ((f32[384,256,1]{0,2,1:T(1,128)}), f32[384,256,1]{0,2,1:T(1,128)S(1)}, u32[]{:S(2)}, u32[]{:S(2)}) async-start(f32[384,256,1]{0,2,1:T(1,128)} %copy.70), calls=%async_computation.1 | async-start | bytes 786432 | tf_op jit(solution)/shard_map/all_to_all | solution.py:107
  62.5 1.1 copy.73
  63.6 23.8 %all-to-all-done.1 = f32[384,256,1]{0,2,1:T(1,128)S(1)} async-done(((f32[384,256,1]{0,2,1:T(1,128)}), f32[384,256,1]{0,2,1:T(1,128)S(1)}, u32[]{:S(2)}, u32[]{:S(2)}) %all-to-all-start.1) | async-done | bytes 393248 | tf_op jit(solution)/shard_map/all_to_all | solution.py:107
  87.4 10.3 %all-to-all-start.2 = ((f32[384,256,1]{0,2,1:T(1,128)}), f32[384,256,1]{0,2,1:T(1,128)S(1)}, u32[]{:S(2)}, u32[]{:S(2)}) async-start(f32[384,256,1]{0,2,1:T(1,128)} %copy.73), calls=%async_computation.2 | async-start | bytes 786432 | tf_op jit(solution)/shard_map/all_to_all | solution.py:108
  97.7 0.1 broadcast_multiply_fusion
  97.7 0.1 copy.82
  97.8 0.1 fusion.105
  97.9 0.1 copy.83
  97.9 0.1 dynamic_slice.3
  98.0 0.1 fusion.114
  98.2 0.5 convolution_multiply_fusion.2
  98.7 23.6 %all-to-all-done.2 = f32[384,256,1]{0,2,1:T(1,128)S(1)} async-done(((f32[384,256,1]{0,2,1:T(1,128)}), f32[384,256,1]{0,2,1:T(1,128)S(1)}, u32[]{:S(2)}, u32[]{:S(2)}) %all-to-all-start.2) | async-done | bytes 393248 | tf_op jit(solution)/shard_map/all_to_all | solution.py:108
  122.3 0.5 convolution_multiply_fusion.3
  122.9 0.5 convolution_add_fusion.1
  123.4 0.6 add_bitcast_fusion
  124.0 0.6 convolution_multiply_fusion.1
  124.6 0.6 convolution_multiply_fusion
  125.2 0.6 convolution_subtract_fusion
  125.8 0.6 convolution_add_fusion
  126.3 0.1 multiply_subtract_fusion.2
  126.4 0.4 fusion.20
  126.8 0.4 fusion.21
  127.2 0.4 convolution_subtract_fusion.3
  127.6 0.5 multiply_subtract_fusion
  128.1 0.4 fusion.18
  128.5 0.4 fusion.14
  129.0 0.4 fusion.2
  129.4 0.4 fusion.1
  129.8 0.3 fusion.13
  130.1 0.9 copy.90
  131.0 10.1 %all-to-all-start.3 = ((f32[256,2,128]{0,1,2:T(2,128)}), f32[256,2,128]{0,1,2:T(2,128)S(1)}, u32[]{:S(2)}, u32[]{:S(2)}) async-start(f32[256,2,128]{0,1,2:T(2,128)} %copy.90), calls=%async_computation.3 | async-start | bytes 524288 | tf_op jit(solution)/shard_map/all_to_all | solution.py:133
  141.2 0.9 copy.91
  142.1 19.4 %all-to-all-done.3 = f32[256,2,128]{0,1,2:T(2,128)S(1)} async-done(((f32[256,2,128]{0,1,2:T(2,128)}), f32[256,2,128]{0,1,2:T(2,128)S(1)}, u32[]{:S(2)}, u32[]{:S(2)}) %all-to-all-start.3) | async-done | bytes 262176 | tf_op jit(solution)/shard_map/all_to_all | solution.py:133
  161.4 9.2 %all-to-all-start.4 = ((f32[256,2,128]{0,1,2:T(2,128)}), f32[256,2,128]{0,1,2:T(2,128)S(1)}, u32[]{:S(2)}, u32[]{:S(2)}) async-start(f32[256,2,128]{0,1,2:T(2,128)} %copy.91), calls=%async_computation.4 | async-start | bytes 524288 | tf_op jit(solution)/shard_map/all_to_all | solution.py:134
  170.7 0.3 all-reduce.2.cloned.1.call-start
  170.9 0.2 reshape.214
  171.1 0.9 fusion.38
  172.1 19.0 %all-to-all-done.4 = f32[256,2,128]{0,1,2:T(2,128)S(1)} async-done(((f32[256,2,128]{0,1,2:T(2,128)}), f32[256,2,128]{0,1,2:T(2,128)S(1)}, u32[]{:S(2)}, u32[]{:S(2)}) %all-to-all-start.4) | async-done | bytes 262176 | tf_op jit(solution)/shard_map/all_to_all | solution.py:134
  191.1 0.2 reshape.215
  191.2 0.9 fusion.3
  192.2 0.1 copy.92
  192.3 25.7 %all_to_all.74 = f32[256,128,1]{0,2,1:T(1,128)S(1)} all-to-all(f32[256,128,1]{0,2,1:T(1,128)S(1)} %copy.92), channel_id=1, replica_groups=mesh['seq'=128,'batch'=4] {'seq'}, dimensions={1} | all-to-all | bytes 262144 | tf_op jit(solution)/shard_map/all_to_all | solution.py:139
  218.0 0.7 slice.46
  218.7 0.0 all-reduce.2.cloned.1.call-update
  218.8 0.7 copy.100
  219.5 41.3 %all-reduce.2.cloned.1.call-done = f32[128,128]{0,1:T(8,128)} async-done(((f32[128,128]{0,1:T(8,128)}), f32[128,128]{0,1:T(8,128)}) %all-reduce.2.cloned.1.call-update) | async-done | bytes 65552 | tf_op jit(solution)/shard_map/psum | solution.py:142
  260.8 1.6 copy.94
  (9 shorter events, 0.2 us)
Async XLA Ops:
  7.2 0.9 copy-start.1
  7.2 1.0 copy-start
  9.2 42.6 %all-to-all-start = ((f32[384,128,1]{0,2,1:T(1,128)}), f32[384,128,1]{0,2,1:T(1,128)S(1)}, u32[]{:S(2)}, u32[]{:S(2)}) async-start(f32[384,128,1]{0,2,1:T(1,128)} %reshape.208), calls=%async_computation | async-start | bytes 393216 | tf_op jit(solution)/shard_map/all_to_all | solution.py:90
  55.0 32.4 %all-to-all-start.1 = ((f32[384,256,1]{0,2,1:T(1,128)}), f32[384,256,1]{0,2,1:T(1,128)S(1)}, u32[]{:S(2)}, u32[]{:S(2)}) async-start(f32[384,256,1]{0,2,1:T(1,128)} %copy.70), calls=%async_computation.1 | async-start | bytes 786432 | tf_op jit(solution)/shard_map/all_to_all | solution.py:107
  87.4 34.9 %all-to-all-start.2 = ((f32[384,256,1]{0,2,1:T(1,128)}), f32[384,256,1]{0,2,1:T(1,128)S(1)}, u32[]{:S(2)}, u32[]{:S(2)}) async-start(f32[384,256,1]{0,2,1:T(1,128)} %copy.73), calls=%async_computation.2 | async-start | bytes 786432 | tf_op jit(solution)/shard_map/all_to_all | solution.py:108
  131.0 30.4 %all-to-all-start.3 = ((f32[256,2,128]{0,1,2:T(2,128)}), f32[256,2,128]{0,1,2:T(2,128)S(1)}, u32[]{:S(2)}, u32[]{:S(2)}) async-start(f32[256,2,128]{0,1,2:T(2,128)} %copy.90), calls=%async_computation.3 | async-start | bytes 524288 | tf_op jit(solution)/shard_map/all_to_all | solution.py:133
  161.4 29.6 %all-to-all-start.4 = ((f32[256,2,128]{0,1,2:T(2,128)}), f32[256,2,128]{0,1,2:T(2,128)S(1)}, u32[]{:S(2)}, u32[]{:S(2)}) async-start(f32[256,2,128]{0,1,2:T(2,128)} %copy.91), calls=%async_computation.4 | async-start | bytes 524288 | tf_op jit(solution)/shard_map/all_to_all | solution.py:134
  170.7 90.1 %all-reduce.2.cloned.1.call-start = ((), (), s32[]{:S(2)}) async-start(), calls=%async_computation.6 | async-start | bytes 131072 | tf_op jit(solution)/shard_map/psum | solution.py:142
Sparse Core Ops, SparseCore 0:
  218.9 41.8 all-reduce.1
where the time goes:
time: 270 us; the launch traced here: 269 us
  waiting for transfers between devices  146 us (54%)
  starting transfers between devices  60.3 us (22%)
  blocking collectives  25.7 us (10%)
  between operations  14.4 us (5%)
  matrix products  11.7 us (4%)
  local copies, waits for them, and re-layouts  10 us (4%)
    psum x1, waiting for transfers between devices, body(): filter_grad = lax.psum(partial_grad, 'batch')  41.3 us
    all_to_all x1, blocking collectives, body(): lax.all_to_all(rebuilt, 'seq', split_axis=1, concat_axis=2, tiled=True)  25.7 us
    all_to_all x1, waiting for transfers between devices, body(): lax.all_to_all(real_part, 'seq', split_axis=1, concat_axis=2, tiled=True)  23.8 us
    all_to_all x1, waiting for transfers between devices, body(): lax.all_to_all(imag_part, 'seq', split_axis=1, concat_axis=2, tiled=True)  23.6 us
    all_to_all x1, starting transfers between devices, body(): lax.all_to_all(stacked.reshape(row_count, seq_count, block_len), 'seq', s...  23 us
    all_to_all x1, waiting for transfers between devices, body(): lax.all_to_all(back_real, 'seq', split_axis=2, concat_axis=1, tiled=True)  19.4 us
    all_to_all x1, waiting for transfers between devices, body(): lax.all_to_all(stacked.reshape(row_count, seq_count, block_len), 'seq', s...  19.3 us
    all_to_all x1, waiting for transfers between devices, body(): lax.all_to_all(back_imag, 'seq', split_axis=2, concat_axis=1, tiled=True)  19 us
  transfers between devices with their start and end apart: 6, of which 6 were waited for; matrix products, arithmetic and copies ran while one was open for 2% of the time, Pallas kernels for 0%

commit v1 on v0

v1 whole, which is shorter than its diff:
```python
import numpy as np

import jax
import jax.numpy as jnp
from jax import lax
from jax.sharding import PartitionSpec as P


def contract(pattern, operand, weights):
    return jnp.einsum(
        pattern,
        operand,
        weights,
        precision=lax.Precision.HIGHEST,
        preferred_element_type=jnp.float32,
    )


def freq_pairs(seq_count):
    low = np.arange(seq_count)
    second = np.where(low == 0, seq_count, 2 * seq_count - low)
    return np.stack([low, second], axis=1)


def tables(seq_count, total_len):
    pairs = freq_pairs(seq_count)
    k1 = pairs.reshape(-1)
    index = np.arange(seq_count)
    theta1 = 2.0 * np.pi * np.outer(index, k1) / (2 * seq_count)
    forward_p = np.concatenate([np.cos(theta1), np.sin(theta1)], axis=1)
    theta2 = 2.0 * np.pi * np.outer(index, index) / seq_count
    local = np.concatenate([np.cos(theta2), np.sin(theta2)], axis=1)
    k1_sr = pairs.T.reshape(-1)
    theta3 = 2.0 * np.pi * np.outer(k1_sr, index) / (2 * seq_count)
    inverse_p = np.concatenate([np.cos(theta3), np.sin(theta3)], axis=1) / total_len
    as32 = lambda a: jnp.asarray(a.astype(np.float32))
    return as32(forward_p), as32(local), as32(inverse_p), pairs.astype(np.int32)


def turn(real_part, imag_part, angle, orient):
    cosine = jnp.cos(angle)
    sine = jnp.sin(angle)
    return (
        real_part * cosine - orient * imag_part * sine,
        imag_part * cosine + orient * real_part * sine,
    )


def body(inputs, out_grad, filters):
    seq_count = lax.axis_size("seq")
    batch_count = lax.axis_size("batch")
    me = lax.axis_index("seq")
    mine = lax.axis_index("batch")
    channels = inputs.shape[1]
    length_dev = inputs.shape[2]
    assert length_dev == seq_count
    group = channels // batch_count
    sub = group // batch_count
    assert group * batch_count == channels and sub * batch_count == group
    total_len = 2 * seq_count * length_dev
    forward_p, local, inverse_p, pairs = tables(seq_count, total_len)
    f32 = jnp.float32

    signal = inputs[0].astype(f32).reshape(batch_count, group, length_dev)
    cotangent = out_grad[0].astype(f32).reshape(batch_count, group, length_dev)
    filt = lax.dynamic_index_in_dim(
        filters.reshape(batch_count, batch_count, sub, length_dev), mine, axis=1, keepdims=False
    )
    send = jnp.concatenate([signal, cotangent, filt], axis=1).transpose(2, 0, 1)
    width = 2 * group + sub
    send = send.reshape(seq_count * batch_count, width)
    recv = lax.all_to_all(send, ("seq", "batch"), 0, 0, tiled=True)
    recv = recv.reshape(seq_count, batch_count, width).transpose(1, 2, 0)
    sig_rows = recv[:, :group].reshape(batch_count * group, seq_count)
    cot_rows = recv[:, group : 2 * group].reshape(batch_count * group, seq_count)
    filt_rows = recv[:, 2 * group :].reshape(group, seq_count)
    half = group // 2
    z_real = jnp.concatenate([sig_rows, filt_rows[:half]], axis=0)
    z_imag = jnp.concatenate([cot_rows, filt_rows[half:]], axis=0)
    rows = z_real.shape[0]

    k1_count = 2 * seq_count
    both = contract("ap,pm->am", jnp.concatenate([z_real, z_imag], axis=0), forward_p)
    a_real = both[:rows, :k1_count] + both[rows:, k1_count:]
    a_imag = both[rows:, :k1_count] - both[:rows, k1_count:]
    k1_all = jnp.asarray(pairs.reshape(-1))
    angle = ((me * k1_all) % total_len).astype(f32) * (2.0 * np.pi / total_len)
    a_real, a_imag = turn(a_real, a_imag, angle[None, :], -1.0)
    stacked = jnp.stack([a_real, a_imag]).reshape(2, rows, seq_count, 2)
    cols = lax.all_to_all(stacked, "seq", 2, 2, tiled=True)

    cols = cols.transpose(0, 1, 3, 2).reshape(2 * rows * 2, seq_count)
    spec = contract("aj,jm->am", cols, local).reshape(2, rows, 2, 2 * seq_count)
    z_re = spec[0, :, :, :seq_count] + spec[1, :, :, seq_count:]
    z_im = spec[1, :, :, :seq_count] - spec[0, :, :, seq_count:]

    flip_re = z_re[:, ::-1, ::-1]
    flip_im = z_im[:, ::-1, ::-1]
    zero_re = jnp.stack([jnp.roll(z_re[:, 0, ::-1], 1, axis=-1), z_re[:, 1, ::-1]], axis=1)
    zero_im = jnp.stack([jnp.roll(z_im[:, 0, ::-1], 1, axis=-1), z_im[:, 1, ::-1]], axis=1)
    at_zero = me == 0
    p_re = jnp.where(at_zero, zero_re, flip_re)
    p_im = -jnp.where(at_zero, zero_im, flip_im)
    first_re = 0.5 * (z_re + p_re)
    first_im = 0.5 * (z_im + p_im)
    second_re = 0.5 * (z_im - p_im)
    second_im = -0.5 * (z_re - p_re)

    sig_count = batch_count * group
    x_re = first_re[:sig_count].reshape(batch_count, group, 2, seq_count)
    x_im = first_im[:sig_count].reshape(batch_count, group, 2, seq_count)
    d_re = second_re[:sig_count].reshape(batch_count, group, 2, seq_count)
    d_im = second_im[:sig_count].reshape(batch_count, group, 2, seq_count)
    h_re = jnp.concatenate([first_re[sig_count:], second_re[sig_count:]], axis=0)
    h_im = jnp.concatenate([first_im[sig_count:], second_im[sig_count:]], axis=0)

    gx_re = h_re * d_re + h_im * d_im
    gx_im = h_re * d_im - h_im * d_re
    gh_re = jnp.sum(x_re * d_re + x_im * d_im, axis=0)
    gh_im = jnp.sum(x_re * d_im - x_im * d_re, axis=0)
    gx_re = gx_re.reshape(sig_count, 2, seq_count)
    gx_im = gx_im.reshape(sig_count, 2, seq_count)
    sig_half = sig_count // 2
    q_re = jnp.concatenate([gx_re[:sig_half] - gx_im[sig_half:], gh_re[:half] - gh_im[half:]], axis=0)
    q_im = jnp.concatenate([gx_im[:sig_half] + gx_re[sig_half:], gh_im[:half] + gh_re[half:]], axis=0)
    back_rows = q_re.shape[0]

    both = contract(
        "ak,km->am", jnp.concatenate([q_re, q_im], axis=0).reshape(2 * back_rows * 2, seq_count), local
    ).reshape(2, back_rows, 2, 2 * seq_count)
    b_re = both[0, :, :, :seq_count] - both[1, :, :, seq_count:]
    b_im = both[1, :, :, :seq_count] + both[0, :, :, seq_count:]
    held = lax.dynamic_index_in_dim(jnp.asarray(pairs), me, axis=0, keepdims=False)
    j_index = jnp.arange(seq_count, dtype=jnp.int32)
    angle = ((held[:, None] * j_index[None, :]) % total_len).astype(f32) * (2.0 * np.pi / total_len)
    b_re, b_im = turn(b_re, b_im, angle[None], 1.0)
    gathered = lax.all_to_all(jnp.stack([b_re, b_im]), "seq", 3, 3, tiled=True)

    out = contract("ak,km->am", gathered.reshape(2 * back_rows, 2 * seq_count), inverse_p)
    out_re = out[:back_rows, :seq_count] - out[back_rows:, seq_count:]
    out_im = out[back_rows:, :seq_count] + out[:back_rows, seq_count:]
    in_rows = jnp.concatenate([out_re[:sig_half], out_im[:sig_half]], axis=0)
    filt_out = jnp.concatenate([out_re[sig_half:], out_im[sig_half:]], axis=0)

    ig = in_rows.reshape(batch_count, group, seq_count).transpose(2, 0, 1)
    fg = jnp.broadcast_to(filt_out.T[:, None, :], (seq_count, batch_count, group))
    send = jnp.concatenate([ig, fg], axis=2).reshape(seq_count * batch_count, 2 * group)
    recv = lax.all_to_all(send, ("seq", "batch"), 0, 0, tiled=True)
    recv = recv.reshape(seq_count, batch_count, 2 * group).transpose(1, 2, 0)
    in_grad = recv[:, :group].reshape(channels, seq_count)
    filter_grad = recv[:, group:].reshape(channels, seq_count)
    return (in_grad.astype(jnp.bfloat16)[None], filter_grad)


def solution(mesh):
    placed = (P("batch", None, "seq"), P("batch", None, "seq"), P(None, "seq"))
    return jax.shard_map(
        body,
        mesh=mesh,
        in_specs=placed,
        out_specs=(P("batch", None, "seq"), P(None, "seq")),
        check_vma=False,
    )
```

time: 270 us -> 172 us (0.64)
  waiting for transfers between devices: 146 us -> 54.1 us
  blocking collectives: 25.7 us -> 69.1 us
  starting transfers between devices: 60.3 us -> 30.6 us
  between operations: 14.4 us -> 1.11 us
  matrix products: 11.7 us -> 1.95 us
    all_to_all x5 -> x2, waiting for transfers between devices: 105 us -> 54.1 us  [the longest x1 30.2 us: body(): cols = lax.all_to_all(stacked, 'seq', 2, 2, tiled=True)]
    all_to_all x1 -> x2, blocking collectives: 25.7 us -> 69.1 us  [the longest x1 37.4 us: body(): recv = lax.all_to_all(send, ('seq', 'batch'), 0, 0, tiled=True)]
    psum x1 -> x0, waiting for transfers between devices: 41.3 us -> none  [body(): filter_grad = lax.psum(partial_grad, 'batch')]
    all_to_all x5 -> x2, starting transfers between devices: 60 us -> 30.6 us  [the longest x1 24.3 us: body(): recv = lax.all_to_all(send, ('seq', 'batch'), 0, 0, tiled=True)]
    dot_general x20 -> x4, matrix products: 11.7 us -> 1.95 us  [contract(): jnp.einsum(pattern, operand, weights, precision=lax.Precision.HIGHEST, pr...]
  transfers between devices with their start and end apart: 6 -> 2, of which waited for: 6 -> 2; matrix products, arithmetic and copies ran while one was open for 2% -> 1% of each run, Pallas kernels for 0% -> 0%
where the time goes in v1:
time: 172 us
  blocking collectives  69.1 us (40%)
  waiting for transfers between devices  54.1 us (31%)
  starting transfers between devices  30.6 us (18%)
  local copies, waits for them, and re-layouts  12.7 us (7%)
  other arithmetic  2.23 us (1%)
  matrix products  1.95 us (1%)
    all_to_all x1, blocking collectives, body(): recv = lax.all_to_all(send, ('seq', 'batch'), 0, 0, tiled=True)  37.4 us
    all_to_all x1, blocking collectives, body(): gathered = lax.all_to_all(jnp.stack([b_re, b_im]), 'seq', 3, 3, tiled=True)  31.7 us
    all_to_all x1, waiting for transfers between devices, body(): cols = lax.all_to_all(stacked, 'seq', 2, 2, tiled=True)  30.2 us
    all_to_all x1, starting transfers between devices, body(): recv = lax.all_to_all(send, ('seq', 'batch'), 0, 0, tiled=True)  24.3 us
    all_to_all x1, waiting for transfers between devices, body(): recv = lax.all_to_all(send, ('seq', 'batch'), 0, 0, tiled=True)  23.9 us
    all_to_all x1, starting transfers between devices, body(): cols = lax.all_to_all(stacked, 'seq', 2, 2, tiled=True)  6.33 us
    unnamed x14, local copies, waits for them, and re-layouts  4.21 us
  transfers between devices with their start and end apart: 2, of which 2 were waited for; matrix products, arithmetic and copies ran while one was open for 1% of the time, Pallas kernels for 0%

profile of v1, /device:TPU:1, one launch (start us, length us, event | category | flops | bytes accessed | tf_op | source)
XLA Modules:
  0.0 171.8 jit_solution(17519832671351387417)
XLA Ops:
  0.6 0.0 copy-start
  0.6 0.8 copy-done
  1.5 0.0 copy-start.4
  1.5 0.1 copy.56
  1.6 0.6 copy-done.4
  2.2 0.0 copy-start.5
  2.2 0.1 copy.57
  2.4 0.6 copy-done.5
  3.0 0.1 copy.58
  3.1 1.0 pad_maximum_fusion.1
  4.2 24.3 %all-to-all-start = ((f32[512,1,72]{2,1,0:T(1,128)}), f32[512,1,72]{2,1,0:T(1,128)S(1)}, u32[]{:S(2)}, u32[]{:S(2)}) async-start(f32[512,1,72]{2,1,0:T(1,128)} %bitcast.6), calls=%async_computation | async-start | bytes 524288 | tf_op jit(solution)/shard_map/all_to_all | solution.py:72
  28.5 0.0 copy-start.6
  28.5 0.7 copy-done.6
  29.2 0.1 fusion.27
  29.3 23.9 %all-to-all-done = f32[512,1,72]{2,1,0:T(1,128)S(1)} async-done(((f32[512,1,72]{2,1,0:T(1,128)}), f32[512,1,72]{2,1,0:T(1,128)S(1)}, u32[]{:S(2)}, u32[]{:S(2)}) %all-to-all-start) | async-done | bytes 147488 | tf_op jit(solution)/shard_map/all_to_all | solution.py:72
  53.2 0.2 fusion.29
  53.4 0.3 fusion.30
  53.7 0.1 copy.62
  53.8 0.0 copy-start.3
  53.8 0.1 copy.60
  53.9 0.1 copy.61
  54.0 0.1 copy.63
  54.1 0.7 copy-done.3
  54.8 0.6 fusion.9
  55.5 0.1 copy.64
  55.6 0.1 stack.26
  55.8 0.1 copy.65
  55.9 0.1 stack.27
  56.1 0.3 pad_maximum_fusion
  56.3 1.0 copy.66
  57.3 6.3 %all-to-all-start.1 = ((f32[2,144,128,2]{1,3,0,2:T(2,128)}), f32[2,144,128,2]{1,3,0,2:T(2,128)S(1)}, u32[]{:S(2)}, u32[]{:S(2)}) async-start(f32[2,144,128,2]{1,3,0,2:T(2,128)} %copy.66), calls=%async_computation.1 | async-start | bytes 1048576 | tf_op jit(solution)/shard_map/all_to_all | solution.py:90
  63.6 0.7 dynamic-slice_bitcast_fusion
  64.3 0.1 fusion.25
  64.4 0.0 copy-start.1
  64.5 30.2 %all-to-all-done.1 = f32[2,144,128,2]{1,3,0,2:T(2,128)S(1)} async-done(((f32[2,144,128,2]{1,3,0,2:T(2,128)}), f32[2,144,128,2]{1,3,0,2:T(2,128)S(1)}, u32[]{:S(2)}, u32[]{:S(2)}) %all-to-all-start.1) | async-done | bytes 294944 | tf_op jit(solution)/shard_map/all_to_all | solution.py:90
  94.7 0.2 copy.67
  94.9 0.0 copy-done.1
  95.0 0.6 fusion
  95.6 0.5 rev.20
  96.2 0.5 rev.23
  96.7 0.3 rev.21
  96.9 0.1 slice.236
  97.0 0.3 rev.18
  97.3 0.1 slice.229
  97.4 0.3 rev.19
  97.7 0.3 rev.22
  97.9 0.1 maximum_bitcast_fusion.1
  98.0 0.1 maximum_bitcast_fusion
  98.1 0.1 subtract_multiply_fusion
  98.4 0.1 subtract_reduce_fusion
  98.5 0.4 fusion.5
  99.0 0.2 copy.69
  99.2 31.7 %all_to_all.28 = f32[2,80,2,128]{1,2,0,3:T(2,128)S(1)} all-to-all(f32[2,80,2,128]{1,2,0,3:T(2,128)S(1)} %copy.69), channel_id=1, replica_groups=mesh['seq'=128,'batch'=4] {'seq'}, dimensions={3} | all-to-all | bytes 327680 | tf_op jit(solution)/shard_map/all_to_all | solution.py:137
  130.8 0.0 copy-start.2
  130.8 0.2 copy.70
  131.0 0.8 copy-done.2
  131.8 0.3 fusion.2
  132.2 0.1 copy.71
  132.3 0.1 copy.72
  132.5 0.2 pad_maximum_fusion.2
  132.7 37.4 %all_to_all.29 = f32[512,1,64]{2,1,0:T(1,128)S(1)} all-to-all(f32[512,1,64]{2,1,0:T(1,128)S(1)} %bitcast.80), channel_id=1, replica_groups=mesh['seq'=128,'batch'=4] {'seq','batch'}, dimensions={0} | all-to-all | bytes 262144 | tf_op jit(solution)/shard_map/all_to_all | solution.py:148
  170.1 0.2 slice.267
  170.4 0.7 copy.75
  171.1 0.7 copy.74
  (31 shorter events, 0.5 us)
Async XLA Ops:
  0.6 0.8 copy-start
  1.5 0.8 copy-start.4
  2.2 0.8 copy-start.5
  4.2 49.0 %all-to-all-start = ((f32[512,1,72]{2,1,0:T(1,128)}), f32[512,1,72]{2,1,0:T(1,128)S(1)}, u32[]{:S(2)}, u32[]{:S(2)}) async-start(f32[512,1,72]{2,1,0:T(1,128)} %bitcast.6), calls=%async_computation | async-start | bytes 524288 | tf_op jit(solution)/shard_map/all_to_all | solution.py:72
  28.5 0.7 copy-start.6
  53.8 1.0 copy-start.3
  57.3 37.4 %all-to-all-start.1 = ((f32[2,144,128,2]{1,3,0,2:T(2,128)}), f32[2,144,128,2]{1,3,0,2:T(2,128)S(1)}, u32[]{:S(2)}, u32[]{:S(2)}) async-start(f32[2,144,128,2]{1,3,0,2:T(2,128)} %copy.66), calls=%async_computation.1 | async-start | bytes 1048576 | tf_op jit(solution)/shard_map/all_to_all | solution.py:90
  64.4 30.5 %copy-start.1 = (f32[128,256,1,1]{1,0,3,2:T(8,128)S(1)}, f32[128,256,1,1]{1,0,3,2:T(8,128)}, u32[]{:S(2)}) copy-start(f32[128,256,1,1]{1,0,3,2:T(8,128)} %constant.71) | copy-start | bytes 393220
  130.8 1.0 copy-start.2

commit v2 on v1

v2 whole, which is shorter than its diff:
```python
import numpy as np

import jax
import jax.numpy as jnp
from jax import lax
from jax.sharding import PartitionSpec as P


def contract(left, right):
    return jnp.matmul(
        left, right, precision=lax.Precision.HIGHEST, preferred_element_type=jnp.float32
    )


def tables(outer, inner, used):
    total = outer * inner
    k1 = np.arange(outer)
    theta1 = 2.0 * np.pi * np.outer(k1, np.arange(used)) / outer
    first = np.concatenate([np.cos(theta1), np.sin(theta1)], axis=0)
    back = np.concatenate([np.cos(theta1).T, np.sin(theta1).T], axis=0) / total
    phi = 2.0 * np.pi * np.outer(k1, np.arange(inner)) / total
    k2 = np.arange(inner)
    theta2 = 2.0 * np.pi * np.outer(k2, k2) / inner
    second = np.concatenate([np.cos(theta2), np.sin(theta2)], axis=1)
    as32 = lambda a: jnp.asarray(a.astype(np.float32))
    return as32(first), as32(back), as32(np.cos(phi)), as32(np.sin(phi)), as32(second)


def partner(values):
    flipped = jnp.roll(values[::-1, ::-1], 1, axis=0)
    row0 = jnp.roll(values[0, ::-1], 1)
    return flipped.at[0].set(row0)


def body(inputs, out_grad, filters):
    seq_count = lax.axis_size("seq")
    batch_count = lax.axis_size("batch")
    mine = lax.axis_index("batch")
    channels = inputs.shape[1]
    length_dev = inputs.shape[2]
    assert channels == seq_count and inputs.shape[0] == 1
    length = seq_count * length_dev
    total = 2 * length
    inner = 2 * length_dev
    outer = total // inner
    used = length // inner
    first, back, tw_cos, tw_sin, second = tables(outer, inner, used)
    f32 = jnp.float32

    send = jnp.stack([inputs[0].astype(f32), out_grad[0].astype(f32), filters], axis=1)
    recv = lax.all_to_all(send, "seq", 0, 0, tiled=True)
    signal = recv[:, 0].reshape(used, inner)
    cotangent = recv[:, 1].reshape(used, inner)
    filt = recv[:, 2].reshape(used, inner)

    stage = contract(first, jnp.concatenate([signal, cotangent, filt], axis=1))
    cos_part, sin_part = stage[:outer], stage[outer:]
    z_re = cos_part[:, :inner] + sin_part[:, inner : 2 * inner]
    z_im = cos_part[:, inner : 2 * inner] - sin_part[:, :inner]
    h_re = cos_part[:, 2 * inner :]
    h_im = -sin_part[:, 2 * inner :]

    def twist(re, im, orient):
        return re * tw_cos - orient * im * tw_sin, im * tw_cos + orient * re * tw_sin

    z_re, z_im = twist(z_re, z_im, -1.0)
    h_re, h_im = twist(h_re, h_im, -1.0)

    stage = contract(jnp.concatenate([z_re, z_im, h_re, h_im], axis=0), second)
    c2, s2 = stage[:, :inner], stage[:, inner:]
    zr = c2[:outer] + s2[outer : 2 * outer]
    zi = c2[outer : 2 * outer] - s2[:outer]
    hr = c2[2 * outer : 3 * outer] + s2[3 * outer :]
    hi = c2[3 * outer :] - s2[2 * outer : 3 * outer]

    pr = partner(zr)
    pi = -partner(zi)
    xr = 0.5 * (zr + pr)
    xi = 0.5 * (zi + pi)
    dr = 0.5 * (zi - pi)
    di = -0.5 * (zr - pr)

    gx_re = hr * dr + hi * di
    gx_im = hr * di - hi * dr
    gh_re = xr * dr + xi * di
    gh_im = xr * di - xi * dr
    q_re = gx_re - gh_im
    q_im = gx_im + gh_re

    stage = contract(jnp.concatenate([q_re, q_im], axis=0), second)
    c2, s2 = stage[:, :inner], stage[:, inner:]
    g_re = c2[:outer] - s2[outer:]
    g_im = c2[outer:] + s2[:outer]
    g_re, g_im = twist(g_re, g_im, 1.0)
    stage = contract(back, jnp.concatenate([g_re, g_im], axis=1))
    c1, s1 = stage[:used], stage[used:]
    in_row = c1[:, :inner] - s1[:, inner:]
    filt_row = c1[:, inner:] + s1[:, :inner]

    in_blocks = in_row.reshape(seq_count, length_dev)
    filt_blocks = filt_row.reshape(seq_count, length_dev)
    own = (jnp.arange(batch_count) == mine)[None, :, None]
    send = jnp.concatenate(
        [
            jnp.where(own, in_blocks[:, None, :], 0.0),
            jnp.broadcast_to(filt_blocks[:, None, :], (seq_count, batch_count, length_dev)),
        ],
        axis=2,
    ).reshape(seq_count * batch_count, 2 * length_dev)
    recv = lax.all_to_all(send, ("seq", "batch"), 0, 0, tiled=True)
    recv = recv.reshape(seq_count, batch_count, 2 * length_dev)
    in_grad = lax.dynamic_index_in_dim(recv[:, :, :length_dev], mine, axis=1, keepdims=False)
    parts = recv[:, :, length_dev:]
    filter_grad = parts[:, 0]
    for index in range(1, batch_count):
        filter_grad = filter_grad + parts[:, index]
    return (in_grad.astype(jnp.bfloat16)[None], filter_grad)


def solution(mesh):
    placed = (P("batch", None, "seq"), P("batch", None, "seq"), P(None, "seq"))
    return jax.shard_map(
        body,
        mesh=mesh,
        in_specs=placed,
        out_specs=(P("batch", None, "seq"), P(None, "seq")),
        check_vma=False,
    )
```

time: 172 us -> 112 us (0.65)
  blocking collectives: 69.1 us -> 0 us
  starting transfers between devices: 30.6 us -> 35 us
  local copies, waits for them, and re-layouts: 12.7 us -> 9.16 us
  waiting for transfers between devices: 54.1 us -> 57.6 us
  other arithmetic: 2.23 us -> 5.63 us
    all_to_all x2 -> x0, blocking collectives: 69.1 us -> none  [the longest x1 37.4 us: body(): recv = lax.all_to_all(send, ('seq', 'batch'), 0, 0, tiled=True)]
    all_to_all x1, starting transfers between devices: 6.33 us -> 23 us  [body(): recv = lax.all_to_all(send, 'seq', 0, 0, tiled=True)]
    all_to_all x1, starting transfers between devices: 24.3 us -> 12 us  [body(): recv = lax.all_to_all(send, ('seq', 'batch'), 0, 0, tiled=True)]
    all_to_all x1, waiting for transfers between devices: 23.9 us -> 35.9 us  [body(): recv = lax.all_to_all(send, ('seq', 'batch'), 0, 0, tiled=True)]
    all_to_all x1, waiting for transfers between devices: 30.2 us -> 21.7 us  [body(): recv = lax.all_to_all(send, 'seq', 0, 0, tiled=True)]
    rev x6 -> x0, local copies, waits for them, and re-layouts: 2.06 us -> none  [the longest x1 0.5 us: body(): flip_re = z_re[:, ::-1, ::-1]]
    unnamed x14 -> x19, local copies, waits for them, and re-layouts: 4.21 us -> 4.73 us
  transfers between devices with their start and end apart: 2 -> 2, of which waited for: 2 -> 2; matrix products, arithmetic and copies ran while one was open for 1% -> 0% of each run, Pallas kernels for 0% -> 0%
where the time goes in v2:
time: 112 us; the launch traced here: 111 us
  waiting for transfers between devices  57.6 us (51%)
  starting transfers between devices  35 us (31%)
  local copies, waits for them, and re-layouts  9.16 us (8%)
  other arithmetic  5.63 us (5%)
  matrix products  2.76 us (2%)
    all_to_all x1, waiting for transfers between devices, body(): recv = lax.all_to_all(send, ('seq', 'batch'), 0, 0, tiled=True)  35.9 us
    all_to_all x1, starting transfers between devices, body(): recv = lax.all_to_all(send, 'seq', 0, 0, tiled=True)  23 us
    all_to_all x1, waiting for transfers between devices, body(): recv = lax.all_to_all(send, 'seq', 0, 0, tiled=True)  21.7 us
    all_to_all x1, starting transfers between devices, body(): recv = lax.all_to_all(send, ('seq', 'batch'), 0, 0, tiled=True)  12 us
    unnamed x19, local copies, waits for them, and re-layouts  4.73 us
    dot_general x4, matrix products, contract(): jnp.matmul(left, right, precision=lax.Precision.HIGHEST, preferred_elemen...  2.76 us
  transfers between devices with their start and end apart: 2, of which 2 were waited for; matrix products, arithmetic and copies ran while one was open for 0% of the time, Pallas kernels for 0%

profile of v2, /device:TPU:1, one launch (start us, length us, event | category | flops | bytes accessed | tf_op | source)
XLA Modules:
  0.0 111.1 jit_solution(15220108507383579252)
XLA Ops:
  0.6 0.0 copy-start.6
  0.6 0.8 convert_element_type.45
  1.4 0.0 copy-done.6
  1.4 0.0 copy-start.4
  1.4 0.8 copy-done.4
  2.3 0.9 pad_maximum_fusion.1
  3.1 23.0 %all-to-all-start = ((f32[128,3,128]{2,1,0:T(4,128)}), f32[128,3,128]{2,1,0:T(4,128)S(1)}, u32[]{:S(2)}, u32[]{:S(2)}) async-start(f32[128,3,128]{2,1,0:T(4,128)} %pad_maximum_fusion.1), calls=%async_computation | async-start | bytes 524288 | tf_op jit(solution)/shard_map/all_to_all | solution.py:51
  26.1 0.1 broadcast_in_dim.38
  26.2 21.7 %all-to-all-done = f32[128,3,128]{2,1,0:T(4,128)S(1)} async-done(((f32[128,3,128]{2,1,0:T(4,128)}), f32[128,3,128]{2,1,0:T(4,128)S(1)}, u32[]{:S(2)}, u32[]{:S(2)}) %all-to-all-start) | async-done | bytes 196640 | tf_op jit(solution)/shard_map/all_to_all | solution.py:51
  47.9 0.5 slice_reduce_fusion.2
  48.5 0.0 copy-start.3
  48.5 0.8 copy-done.3
  49.4 0.0 copy-start.1
  49.4 0.0 copy-start.2
  49.4 0.8 fusion.16
  50.2 0.1 copy-done.1
  50.3 0.1 copy-done.2
  50.4 0.0 copy-start
  50.4 0.1 multiply_subtract_fusion.2
  50.4 0.9 copy-done
  51.4 1.0 fusion
  52.5 0.1 slice.285
  52.5 0.5 slice.284
  53.1 0.1 slice.293
  53.1 0.5 slice.292
  53.7 0.2 reverse.9
  53.9 0.1 slice.394
  54.0 0.3 slice.237
  54.2 0.2 slice.235
  54.4 0.2 reverse.8
  54.6 0.1 slice.393
  54.7 0.3 slice.250
  54.9 0.2 slice.248
  55.2 0.7 pad_maximum_fusion.4
  55.9 0.7 pad_maximum_fusion.5
  56.7 0.1 subtract_subtract_fusion
  56.9 0.6 fusion.8
  57.5 0.0 copy-start.5
  57.5 0.1 multiply_subtract_fusion
  57.6 0.8 copy-done.5
  58.3 0.4 fusion.12
  58.8 0.1 broadcast_select_fusion
  59.0 1.1 %all_to_all.10 = f32[512,1,256]{2,1,0:T(1,128)} reshape(f32[512,256]{1,0:T(8,128)S(1)} %pad_maximum_fusion) | data formatting | bytes 1048576 | tf_op jit(solution)/shard_map/all_to_all | solution.py:110
  60.2 12.0 %all-to-all-start.1 = ((f32[512,1,256]{2,1,0:T(1,128)}), f32[512,1,256]{2,1,0:T(1,128)S(1)}, u32[]{:S(2)}, u32[]{:S(2)}) async-start(f32[512,1,256]{2,1,0:T(1,128)} %all_to_all.10), calls=%async_computation.1 | async-start | bytes 1048576 | tf_op jit(solution)/shard_map/all_to_all | solution.py:110
  72.2 35.9 %all-to-all-done.1 = f32[512,1,256]{2,1,0:T(1,128)S(1)} async-done(((f32[512,1,256]{2,1,0:T(1,128)}), f32[512,1,256]{2,1,0:T(1,128)S(1)}, u32[]{:S(2)}, u32[]{:S(2)}) %all-to-all-start.1) | async-done | bytes 524320 | tf_op jit(solution)/shard_map/all_to_all | solution.py:110
  108.1 1.2 %reduce.7 = f32[512,256]{1,0:T(8,128)S(1)} reduce(f32[512,1,256]{2,1,0:T(1,128)S(1)} %all-to-all-done.1, f32[]{:T(128)} %constant.85), dimensions={1}, to_apply=%all_to_all.11.reduce_sub_computation | reduce | bytes 1048580 | tf_op jit(solution)/shard_map/all_to_all | solution.py:110
  109.4 0.1 reshape.116
  109.6 0.8 slice_add_fusion.4
  110.4 0.1 dynamic-slice_convert_fusion
  110.4 0.6 copy.13
  (22 shorter events, 0.5 us)
Async XLA Ops:
  0.6 0.8 copy-start.6
  1.4 0.8 copy-start.4
  3.1 44.8 %all-to-all-start = ((f32[128,3,128]{2,1,0:T(4,128)}), f32[128,3,128]{2,1,0:T(4,128)S(1)}, u32[]{:S(2)}, u32[]{:S(2)}) async-start(f32[128,3,128]{2,1,0:T(4,128)} %pad_maximum_fusion.1), calls=%async_computation | async-start | bytes 524288 | tf_op jit(solution)/shard_map/all_to_all | solution.py:51
  48.5 0.9 copy-start.3
  49.4 0.9 copy-start.1
  49.4 1.0 copy-start.2
  50.4 1.0 copy-start
  57.5 0.8 copy-start.5
  60.2 47.9 %all-to-all-start.1 = ((f32[512,1,256]{2,1,0:T(1,128)}), f32[512,1,256]{2,1,0:T(1,128)S(1)}, u32[]{:S(2)}, u32[]{:S(2)}) async-start(f32[512,1,256]{2,1,0:T(1,128)} %all_to_all.10), calls=%async_computation.1 | async-start | bytes 1048576 | tf_op jit(solution)/shard_map/all_to_all | solution.py:110

commit v3 on v2

--- a/solution.py
+++ b/solution.py
@@ -97,23 +97,19 @@
     in_row = c1[:, :inner] - s1[:, inner:]
     filt_row = c1[:, inner:] + s1[:, :inner]
 
-    in_blocks = in_row.reshape(seq_count, length_dev)
-    filt_blocks = filt_row.reshape(seq_count, length_dev)
-    own = (jnp.arange(batch_count) == mine)[None, :, None]
+    assert batch_count & (batch_count - 1) == 0
+    step = 1
+    while step < batch_count:
+        pairs = [(index, index ^ step) for index in range(batch_count)]
+        filt_row = filt_row + lax.ppermute(filt_row, "batch", pairs)
+        step *= 2
+
     send = jnp.concatenate(
-        [
-            jnp.where(own, in_blocks[:, None, :], 0.0),
-            jnp.broadcast_to(filt_blocks[:, None, :], (seq_count, batch_count, length_dev)),
-        ],
-        axis=2,
-    ).reshape(seq_count * batch_count, 2 * length_dev)
-    recv = lax.all_to_all(send, ("seq", "batch"), 0, 0, tiled=True)
-    recv = recv.reshape(seq_count, batch_count, 2 * length_dev)
-    in_grad = lax.dynamic_index_in_dim(recv[:, :, :length_dev], mine, axis=1, keepdims=False)
-    parts = recv[:, :, length_dev:]
-    filter_grad = parts[:, 0]
-    for index in range(1, batch_count):
-        filter_grad = filter_grad + parts[:, index]
+        [in_row.reshape(seq_count, length_dev), filt_row.reshape(seq_count, length_dev)], axis=1
+    )
+    recv = lax.all_to_all(send, "seq", 0, 0, tiled=True)
+    in_grad = recv[:, :length_dev]
+    filter_grad = recv[:, length_dev:]
     return (in_grad.astype(jnp.bfloat16)[None], filter_grad)
 
 

time: 112 us -> 94.8 us (0.85)
  blocking collectives: 0 us -> 67.1 us
  waiting for transfers between devices: 57.6 us -> 3.57 us
  starting transfers between devices: 35 us -> 8.02 us
  other arithmetic: 5.63 us -> 2.76 us
    all_to_all x0 -> x2, blocking collectives: none -> 67.1 us  [body(): recv = lax.all_to_all(send, 'seq', 0, 0, tiled=True)]
    all_to_all x2 -> x0, waiting for transfers between devices: 57.6 us -> none  [the longest x1 35.9 us: body(): recv = lax.all_to_all(send, ('seq', 'batch'), 0, 0, tiled=True)]
    all_to_all x2 -> x0, starting transfers between devices: 35 us -> none  [the longest x1 23 us: body(): recv = lax.all_to_all(send, 'seq', 0, 0, tiled=True)]
    ppermute x0 -> x2, starting transfers between devices: none -> 8.02 us  [body(): filt_row = filt_row + lax.ppermute(filt_row, 'batch', pairs)]
    ppermute x0 -> x2, waiting for transfers between devices: none -> 3.57 us  [body(): filt_row = filt_row + lax.ppermute(filt_row, 'batch', pairs)]
    all_to_all x1 -> x0, other arithmetic: 1.24 us -> none  [body(): recv = lax.all_to_all(send, ('seq', 'batch'), 0, 0, tiled=True)]
where the time goes in v3:
time: 94.8 us; the launch traced here: 93.3 us
  blocking collectives  67.1 us (71%)
  local copies, waits for them, and re-layouts  8.24 us (9%)
  starting transfers between devices  8.02 us (8%)
  waiting for transfers between devices  3.57 us (4%)
  other arithmetic  2.76 us (3%)
  matrix products  2.76 us (3%)
    all_to_all x2, blocking collectives, body(): recv = lax.all_to_all(send, 'seq', 0, 0, tiled=True)  67.1 us
    ppermute x2, starting transfers between devices, body(): filt_row = filt_row + lax.ppermute(filt_row, 'batch', pairs)  8.02 us
    unnamed x19, local copies, waits for them, and re-layouts  4.12 us
    ppermute x2, waiting for transfers between devices, body(): filt_row = filt_row + lax.ppermute(filt_row, 'batch', pairs)  3.57 us
    dot_general x4, matrix products, contract(): jnp.matmul(left, right, precision=lax.Precision.HIGHEST, preferred_elemen...  2.76 us
  transfers between devices with their start and end apart: 2, of which 2 were waited for; matrix products, arithmetic and copies ran while one was open for 0% of the time, Pallas kernels for 0%

profile of v3, /device:TPU:1, one launch (start us, length us, event | category | flops | bytes accessed | tf_op | source)
XLA Modules:
  0.0 93.3 jit_solution(18349854893633723785)
XLA Ops:
  0.6 0.0 copy-start.6
  0.6 0.8 convert_element_type.31
  1.4 0.0 copy-done.6
  1.4 0.0 copy-start.4
  1.4 0.8 copy-done.4
  2.3 0.2 pad_maximum_fusion
  2.4 44.6 %all_to_all.17 = f32[128,3,128]{2,1,0:T(4,128)S(1)} all-to-all(f32[128,3,128]{2,1,0:T(4,128)S(1)} %pad_maximum_fusion), channel_id=1, replica_groups=mesh['seq'=128,'batch'=4] {'seq'}, dimensions={0} | all-to-all | bytes 393216 | tf_op jit(solution)/shard_map/all_to_all | solution.py:51
  47.0 0.5 slice_reduce_fusion.2
  47.6 0.0 copy-start.3
  47.6 0.8 copy-done.3
  48.5 0.0 copy-start.1
  48.5 0.0 copy-start.2
  48.5 0.8 fusion.16
  49.3 0.1 copy-done.1
  49.4 0.1 copy-done.2
  49.4 0.0 copy-start
  49.5 0.1 multiply_subtract_fusion.2
  49.5 0.9 %copy-done = f32[256,512]{1,0:T(8,128)S(1)} copy-done((f32[256,512]{1,0:T(8,128)S(1)}, f32[256,512]{1,0:T(8,128)}, u32[]{:S(2)}) %copy-start) | copy-done | bytes 524312
  50.5 1.0 %fusion = f32[512,512]{1,0:T(8,128)S(1)} fusion(f32[256,512]{1,0:T(8,128)S(1)} %copy-done, f32[128,256]{1,0:T(8,128)S(1)} %get-tuple-element.34, f32[128,256]{1,0:T(8,128)S(1)} %get-tuple-element.35, f32[128,256]{1,0:T(8,128)S(1)} %get-tuple-element.36, f32[128,256]{1,0:T(8,128)S(1)} %get-tuple-element.33), kind=kOutput, calls=%fused_computation | convolution fusion | flops 805699584 | bytes 2097152 | tf_op jit(solution)/shard_map/dot_general | solution.py:10
  51.6 0.5 slice.268
  52.1 0.1 slice.269
  52.1 0.5 slice.276
  52.7 0.1 slice.277
  52.8 0.2 reverse.9
  53.0 0.1 slice.370
  53.0 0.2 slice.222
  53.2 0.2 reverse.8
  53.4 0.1 slice.369
  53.5 0.2 slice.235
  53.7 0.3 slice.224
  53.9 0.3 slice.237
  54.2 0.7 pad_maximum_fusion.4
  55.0 0.7 pad_maximum_fusion.5
  55.8 0.1 subtract_subtract_fusion
  55.9 0.6 fusion.8
  56.6 0.0 copy-start.5
  56.6 0.1 multiply_subtract_fusion
  56.6 0.8 copy-done.5
  57.4 0.4 fusion.12
  57.8 5.7 %collective-permute-start = (f32[64,256]{1,0:T(8,128)S(1)}, f32[64,256]{1,0:T(8,128)S(1)}, u32[]{:S(2)}, u32[]{:S(2)}) collective-permute-start(f32[64,256]{1,0:T(8,128)S(1)} %get-tuple-element.40), channel_id=1, source_target_pairs={{0,1},{1,0},{2,3},{3,2},{4,5},{5,4},{6,7},{7,6},{8,9},{9,8},{10,11... | collective-permute-start | bytes 196616 | tf_op jit(solution)/shard_map/ppermute | solution.py:104
  63.5 0.9 collective-permute-done
  64.4 2.3 %collective-permute-start.1 = (f32[64,256]{1,0:T(8,128)S(1)}, f32[64,256]{1,0:T(8,128)S(1)}, u32[]{:S(2)}, u32[]{:S(2)}) collective-permute-start(f32[64,256]{1,0:T(8,128)S(1)} %add.62), channel_id=1, source_target_pairs={{0,2},{1,3},{2,0},{3,1},{4,6},{5,7},{6,4},{7,5},{8,10},{9,11},{10,... | collective-permute-start | bytes 196616 | tf_op jit(solution)/shard_map/ppermute | solution.py:104
  66.7 2.7 %collective-permute-done.1 = f32[64,256]{1,0:T(8,128)S(1)} collective-permute-done((f32[64,256]{1,0:T(8,128)S(1)}, f32[64,256]{1,0:T(8,128)S(1)}, u32[]{:S(2)}, u32[]{:S(2)}) %collective-permute-start.1) | collective-permute-done | bytes 65568 | tf_op jit(solution)/shard_map/ppermute | solution.py:104
  69.5 0.1 all_to_all.12
  69.6 22.5 %all_to_all.18 = f32[128,1,256]{2,1,0:T(1,128)S(1)} all-to-all(f32[128,1,256]{2,1,0:T(1,128)S(1)} %all_to_all.12), channel_id=1, replica_groups=mesh['seq'=128,'batch'=4] {'seq'}, dimensions={0} | all-to-all | bytes 262144 | tf_op jit(solution)/shard_map/all_to_all | solution.py:110
  92.1 0.6 fusion.22
  92.7 0.6 slice.287
  (20 shorter events, 0.3 us)
Async XLA Ops:
  0.6 0.8 copy-start.6
  1.4 0.8 copy-start.4
  47.6 0.9 copy-start.3
  48.5 0.9 copy-start.1
  48.5 1.0 %copy-start.2 = (f32[128,256]{1,0:T(8,128)S(1)}, f32[128,256]{1,0:T(8,128)}, u32[]{:S(2)}) copy-start(f32[128,256]{1,0:T(8,128)} %constant.66.clone) | copy-start | bytes 393220
  49.4 1.0 %copy-start = (f32[256,512]{1,0:T(8,128)S(1)}, f32[256,512]{1,0:T(8,128)}, u32[]{:S(2)}) copy-start(f32[256,512]{1,0:T(8,128)} %constant.68.clone) | copy-start | bytes 1572868
  56.6 0.8 copy-start.5
  57.8 6.6 %collective-permute-start = (f32[64,256]{1,0:T(8,128)S(1)}, f32[64,256]{1,0:T(8,128)S(1)}, u32[]{:S(2)}, u32[]{:S(2)}) collective-permute-start(f32[64,256]{1,0:T(8,128)S(1)} %get-tuple-element.40), channel_id=1, source_target_pairs={{0,1},{1,0},{2,3},{3,2},{4,5},{5,4},{6,7},{7,6},{8,9},{9,8},{10,11... | collective-permute-start | bytes 196616 | tf_op jit(solution)/shard_map/ppermute | solution.py:104
  64.4 5.0 %collective-permute-start.1 = (f32[64,256]{1,0:T(8,128)S(1)}, f32[64,256]{1,0:T(8,128)S(1)}, u32[]{:S(2)}, u32[]{:S(2)}) collective-permute-start(f32[64,256]{1,0:T(8,128)S(1)} %add.62), channel_id=1, source_target_pairs={{0,2},{1,3},{2,0},{3,1},{4,6},{5,7},{6,4},{7,5},{8,10},{9,11},{10,... | collective-permute-start | bytes 196616 | tf_op jit(solution)/shard_map/ppermute | solution.py:104

commit v4 on v3

--- a/solution.py
+++ b/solution.py
@@ -26,12 +26,6 @@
     return as32(first), as32(back), as32(np.cos(phi)), as32(np.sin(phi)), as32(second)
 
 
-def partner(values):
-    flipped = jnp.roll(values[::-1, ::-1], 1, axis=0)
-    row0 = jnp.roll(values[0, ::-1], 1)
-    return flipped.at[0].set(row0)
-
-
 def body(inputs, out_grad, filters):
     seq_count = lax.axis_size("seq")
     batch_count = lax.axis_size("batch")
@@ -55,30 +49,23 @@
 
     stage = contract(first, jnp.concatenate([signal, cotangent, filt], axis=1))
     cos_part, sin_part = stage[:outer], stage[outer:]
-    z_re = cos_part[:, :inner] + sin_part[:, inner : 2 * inner]
-    z_im = cos_part[:, inner : 2 * inner] - sin_part[:, :inner]
-    h_re = cos_part[:, 2 * inner :]
-    h_im = -sin_part[:, 2 * inner :]
 
     def twist(re, im, orient):
         return re * tw_cos - orient * im * tw_sin, im * tw_cos + orient * re * tw_sin
 
-    z_re, z_im = twist(z_re, z_im, -1.0)
-    h_re, h_im = twist(h_re, h_im, -1.0)
+    parts = []
+    for index in range(3):
+        cut = slice(index * inner, (index + 1) * inner)
+        parts.extend(twist(cos_part[:, cut], -sin_part[:, cut], -1.0))
 
-    stage = contract(jnp.concatenate([z_re, z_im, h_re, h_im], axis=0), second)
+    stage = contract(jnp.concatenate(parts, axis=0), second)
     c2, s2 = stage[:, :inner], stage[:, inner:]
-    zr = c2[:outer] + s2[outer : 2 * outer]
-    zi = c2[outer : 2 * outer] - s2[:outer]
-    hr = c2[2 * outer : 3 * outer] + s2[3 * outer :]
-    hi = c2[3 * outer :] - s2[2 * outer : 3 * outer]
-
-    pr = partner(zr)
-    pi = -partner(zi)
-    xr = 0.5 * (zr + pr)
-    xi = 0.5 * (zi + pi)
-    dr = 0.5 * (zi - pi)
-    di = -0.5 * (zr - pr)
+    spectra = []
+    for index in range(3):
+        re_rows = slice(2 * index * outer, (2 * index + 1) * outer)
+        im_rows = slice((2 * index + 1) * outer, (2 * index + 2) * outer)
+        spectra.append((c2[re_rows] + s2[im_rows], c2[im_rows] - s2[re_rows]))
+    (xr, xi), (dr, di), (hr, hi) = spectra
 
     gx_re = hr * dr + hi * di
     gx_im = hr * di - hi * dr

time: 94.8 us -> 90.2 us (0.951)
  local copies, waits for them, and re-layouts: 8.24 us -> 2.92 us
    unnamed x19 -> x11, local copies, waits for them, and re-layouts: 4.12 us -> 1 us
    slice x12 -> x0, local copies, waits for them, and re-layouts: 2.12 us -> none  [the longest x4 1.17 us: partner(): row0 = jnp.roll(values[0, ::-1], 1)]
    concatenate x4 -> x1, other arithmetic: 1.47 us -> 0.04 us  [body(): stage = contract(jnp.concatenate(parts, axis=0), second)]
where the time goes in v4:
time: 90.2 us; the launch traced here: 88.8 us
  blocking collectives  67.1 us (74%)
  starting transfers between devices  8.02 us (9%)
  waiting for transfers between devices  3.56 us (4%)
  other arithmetic  3.15 us (3%)
  matrix products  3.15 us (3%)
  local copies, waits for them, and re-layouts  2.92 us (3%)
    all_to_all x2, blocking collectives, body(): recv = lax.all_to_all(send, 'seq', 0, 0, tiled=True)  67.1 us
    ppermute x2, starting transfers between devices, body(): filt_row = filt_row + lax.ppermute(filt_row, 'batch', pairs)  8.02 us
    ppermute x2, waiting for transfers between devices, body(): filt_row = filt_row + lax.ppermute(filt_row, 'batch', pairs)  3.56 us
    dot_general x4, matrix products, contract(): jnp.matmul(left, right, precision=lax.Precision.HIGHEST, preferred_elemen...  3.15 us
  transfers between devices with their start and end apart: 2, of which 2 were waited for; matrix products, arithmetic and copies ran while one was open for 0% of the time, Pallas kernels for 0%

profile of v4, /device:TPU:1, one launch (start us, length us, event | category | flops | bytes accessed | tf_op | source)
XLA Modules:
  0.0 88.8 jit_solution(2201716672631010076)
XLA Ops:
  0.6 0.0 copy-start.3
  0.6 0.0 copy-start
  0.7 0.0 copy-start.1
  0.7 0.8 convert_element_type.31
  1.5 0.8 convert_element_type.32
  2.2 1.0 %pad_maximum_fusion = f32[128,3,128]{2,1,0:T(4,128)S(1)} fusion(f32[128,1,128]{2,1,0:T(1,128)} %bitcast.17, f32[128,1,128]{2,1,0:T(1,128)S(1)} %bitcast.16, f32[128,1,128]{2,1,0:T(1,128)S(1)} %bitcast.15), kind=kLoop, calls=%fused_computation | loop fusion | flops 98304 | bytes 393216 | tf_op jit(solution)/shard_map/stack | solution.py:44
  3.3 44.6 %all_to_all.17 = f32[128,3,128]{2,1,0:T(4,128)S(1)} all-to-all(f32[128,3,128]{2,1,0:T(4,128)S(1)} %pad_maximum_fusion), channel_id=1, replica_groups=mesh['seq'=128,'batch'=4] {'seq'}, dimensions={0} | all-to-all | bytes 393216 | tf_op jit(solution)/shard_map/all_to_all | solution.py:45
  47.9 0.5 slice_reduce_fusion.2
  48.5 0.0 copy-done.3
  48.5 0.8 fusion.8
  49.3 0.0 copy-done
  49.3 0.0 copy-done.1
  49.3 0.0 copy-start.2
  49.6 0.8 copy-done.2
  50.4 1.4 %fusion.18 = f32[768,512]{1,0:T(8,128)S(1)} fusion(f32[768,256]{1,0:T(8,128)S(1)} %add_dynamic-update-slice_fusion, f32[256,512]{1,0:T(8,128)S(1)} %copy-done.2), kind=kOutput, calls=%fused_computation.48 | convolution fusion | flops 1207959552 | bytes 2883584 | tf_op jit(solution)/shard_map/dot_general | solution.py:10
  51.8 0.1 subtract_subtract_fusion
  51.9 0.1 add_add_fusion
  52.0 0.0 copy-start.4
  52.0 0.6 fusion
  52.6 0.1 multiply_subtract_fusion
  52.7 0.1 copy-done.4
  52.8 0.4 fusion.4
  53.2 5.7 %collective-permute-start = (f32[64,256]{1,0:T(8,128)S(1)}, f32[64,256]{1,0:T(8,128)S(1)}, u32[]{:S(2)}, u32[]{:S(2)}) collective-permute-start(f32[64,256]{1,0:T(8,128)S(1)} %get-tuple-element.8), channel_id=1, source_target_pairs={{0,1},{1,0},{2,3},{3,2},{4,5},{5,4},{6,7},{7,6},{8,9},{9,8},{10,11... | collective-permute-start | bytes 196616 | tf_op jit(solution)/shard_map/ppermute | solution.py:91
  59.0 0.9 collective-permute-done
  59.9 2.3 %collective-permute-start.1 = (f32[64,256]{1,0:T(8,128)S(1)}, f32[64,256]{1,0:T(8,128)S(1)}, u32[]{:S(2)}, u32[]{:S(2)}) collective-permute-start(f32[64,256]{1,0:T(8,128)S(1)} %add.54), channel_id=1, source_target_pairs={{0,2},{1,3},{2,0},{3,1},{4,6},{5,7},{6,4},{7,5},{8,10},{9,11},{10,... | collective-permute-start | bytes 196616 | tf_op jit(solution)/shard_map/ppermute | solution.py:91
  62.2 2.7 %collective-permute-done.1 = f32[64,256]{1,0:T(8,128)S(1)} collective-permute-done((f32[64,256]{1,0:T(8,128)S(1)}, f32[64,256]{1,0:T(8,128)S(1)}, u32[]{:S(2)}, u32[]{:S(2)}) %collective-permute-start.1) | collective-permute-done | bytes 65568 | tf_op jit(solution)/shard_map/ppermute | solution.py:91
  64.9 0.1 all_to_all.12
  65.0 22.5 %all_to_all.18 = f32[128,1,256]{2,1,0:T(1,128)S(1)} all-to-all(f32[128,1,256]{2,1,0:T(1,128)S(1)} %all_to_all.12), channel_id=1, replica_groups=mesh['seq'=128,'batch'=4] {'seq'}, dimensions={0} | all-to-all | bytes 262144 | tf_op jit(solution)/shard_map/all_to_all | solution.py:97
  87.5 0.6 fusion.14
  88.1 0.6 slice.189
  (16 shorter events, 0.4 us)
Async XLA Ops:
  0.6 47.8 %copy-start.3 = (f32[256,64]{1,0:T(8,128)S(1)}, f32[256,64]{1,0:T(8,128)}, u32[]{:S(2)}) copy-start(f32[256,64]{1,0:T(8,128)} %constant.12.clone) | copy-start | bytes 196612
  0.6 48.6 %copy-start = (f32[128,256]{1,0:T(8,128)S(1)}, f32[128,256]{1,0:T(8,128)}, u32[]{:S(2)}) copy-start(f32[128,256]{1,0:T(8,128)} %constant.15.clone) | copy-start | bytes 393220
  0.7 48.6 %copy-start.1 = (f32[128,256]{1,0:T(8,128)S(1)}, f32[128,256]{1,0:T(8,128)}, u32[]{:S(2)}) copy-start(f32[128,256]{1,0:T(8,128)} %constant.14.clone) | copy-start | bytes 393220
  49.3 1.0 %copy-start.2 = (f32[256,512]{1,0:T(8,128)S(1)}, f32[256,512]{1,0:T(8,128)}, u32[]{:S(2)}) copy-start(f32[256,512]{1,0:T(8,128)} %constant.16.clone) | copy-start | bytes 1572868
  52.0 0.8 copy-start.4
  53.2 6.6 %collective-permute-start = (f32[64,256]{1,0:T(8,128)S(1)}, f32[64,256]{1,0:T(8,128)S(1)}, u32[]{:S(2)}, u32[]{:S(2)}) collective-permute-start(f32[64,256]{1,0:T(8,128)S(1)} %get-tuple-element.8), channel_id=1, source_target_pairs={{0,1},{1,0},{2,3},{3,2},{4,5},{5,4},{6,7},{7,6},{8,9},{9,8},{10,11... | collective-permute-start | bytes 196616 | tf_op jit(solution)/shard_map/ppermute | solution.py:91
  59.9 5.0 %collective-permute-start.1 = (f32[64,256]{1,0:T(8,128)S(1)}, f32[64,256]{1,0:T(8,128)S(1)}, u32[]{:S(2)}, u32[]{:S(2)}) collective-permute-start(f32[64,256]{1,0:T(8,128)S(1)} %add.54), channel_id=1, source_target_pairs={{0,2},{1,3},{2,0},{3,1},{4,6},{5,7},{6,4},{7,5},{8,10},{9,11},{10,... | collective-permute-start | bytes 196616 | tf_op jit(solution)/shard_map/ppermute | solution.py:91

commit v5 on v4

--- a/solution.py
+++ b/solution.py
@@ -42,7 +42,9 @@
     f32 = jnp.float32
 
     send = jnp.stack([inputs[0].astype(f32), out_grad[0].astype(f32), filters], axis=1)
+    send = send.reshape(channels, 1, 3 * length_dev)
     recv = lax.all_to_all(send, "seq", 0, 0, tiled=True)
+    recv = recv.reshape(seq_count, 3, length_dev)
     signal = recv[:, 0].reshape(used, inner)
     cotangent = recv[:, 1].reshape(used, inner)
     filt = recv[:, 2].reshape(used, inner)
@@ -84,12 +86,19 @@
     in_row = c1[:, :inner] - s1[:, inner:]
     filt_row = c1[:, inner:] + s1[:, :inner]
 
-    assert batch_count & (batch_count - 1) == 0
-    step = 1
-    while step < batch_count:
+    received = [filt_row]
+    for step in range(1, batch_count):
         pairs = [(index, index ^ step) for index in range(batch_count)]
-        filt_row = filt_row + lax.ppermute(filt_row, "batch", pairs)
-        step *= 2
+        received.append(lax.ppermute(filt_row, "batch", pairs))
+    ordered = []
+    for source in range(batch_count):
+        pick = received[0]
+        for step in range(1, batch_count):
+            pick = jnp.where((mine ^ step) == source, received[step], pick)
+        ordered.append(pick)
+    filt_row = ordered[0]
+    for source in range(1, batch_count):
+        filt_row = filt_row + ordered[source]
 
     send = jnp.concatenate(
         [in_row.reshape(seq_count, length_dev), filt_row.reshape(seq_count, length_dev)], axis=1

time: 90.2 us -> 88.6 us (0.982)
  local copies, waits for them, and re-layouts: 2.92 us -> 5.71 us
  starting transfers between devices: 8.02 us -> 10.6 us
  other arithmetic: 3.15 us -> 0.6 us
  waiting for transfers between devices: 3.56 us -> 1.17 us
  blocking collectives: 67.1 us -> 65.8 us
    unnamed x11 -> x14, local copies, waits for them, and re-layouts: 1 us -> 3.7 us
    ppermute x2 -> x3, starting transfers between devices: 8.02 us -> 10.6 us  [body(): received.append(lax.ppermute(filt_row, 'batch', pairs))]
    ppermute x2 -> x3, waiting for transfers between devices: 3.56 us -> 1.17 us  [body(): received.append(lax.ppermute(filt_row, 'batch', pairs))]
    all_to_all x2, blocking collectives: 67.1 us -> 65.8 us  [body(): recv = lax.all_to_all(send, 'seq', 0, 0, tiled=True)]
    another operation x1, other arithmetic: 1.02 us -> 0.02 us  [body(): jnp.stack([inputs[0].astype(f32), out_grad[0].astype(f32), filters], axis=1)]
  transfers between devices with their start and end apart: 2 -> 3, of which waited for: 2 -> 2; matrix products, arithmetic and copies ran while one was open for 0% -> 0% of each run, Pallas kernels for 0% -> 0%
where the time goes in v5:
time: 88.6 us; the launch traced here: 88 us
  blocking collectives  65.8 us (74%)
  starting transfers between devices  10.6 us (12%)
  local copies, waits for them, and re-layouts  5.71 us (6%)
  matrix products  3.16 us (4%)
  waiting for transfers between devices  1.17 us (1%)
  between operations  0.97 us (1%)
    all_to_all x2, blocking collectives, body(): recv = lax.all_to_all(send, 'seq', 0, 0, tiled=True)  65.8 us
    ppermute x3, starting transfers between devices, body(): received.append(lax.ppermute(filt_row, 'batch', pairs))  10.6 us
    unnamed x14, local copies, waits for them, and re-layouts  3.7 us
    dot_general x4, matrix products, contract(): jnp.matmul(left, right, precision=lax.Precision.HIGHEST, preferred_elemen...  3.16 us
  transfers between devices with their start and end apart: 3, of which 2 were waited for; matrix products, arithmetic and copies ran while one was open for 0% of the time, Pallas kernels for 0%

profile of v5, /device:TPU:1, one launch (start us, length us, event | category | flops | bytes accessed | tf_op | source)
XLA Modules:
  0.0 88.0 jit_solution(2269319841801743244)
XLA Ops:
  0.6 0.9 copy.19
  1.5 0.0 copy-start.3
  1.5 0.9 %copy.20 = bf16[1,128,128]{1,2,0:T(8,128)(2,1)S(1)} copy(bf16[1,128,128]{2,1,0:T(8,128)(2,1)} %param.9) | data formatting | bytes 65536 | tf_op args[1]
  2.4 0.9 %copy.21 = f32[128,128]{0,1:T(8,128)S(1)} copy(f32[128,128]{1,0:T(8,128)} %param.10) | data formatting | bytes 131072 | tf_op args[2]
  3.4 0.2 copy.22
  3.6 0.0 copy-start
  3.6 0.0 copy-start.1
  3.6 42.4 %all_to_all.17 = f32[128,1,384]{2,1,0:T(1,128)S(1)} all-to-all(f32[128,1,384]{2,1,0:T(1,128)S(1)} %copy.22), channel_id=1, replica_groups=mesh['seq'=128,'batch'=4] {'seq'}, dimensions={0} | all-to-all | bytes 393216 | tf_op jit(solution)/shard_map/all_to_all | solution.py:46
  46.0 0.2 copy.23
  46.2 0.1 copy.25
  46.3 0.1 copy.26
  46.4 0.1 copy.24
  46.6 0.0 copy-done.3
  46.6 0.8 fusion.8
  47.4 0.0 copy-done
  47.4 0.0 copy-done.1
  47.4 0.0 copy-start.2
  47.7 0.8 copy-done.2
  48.5 1.4 %fusion.19 = f32[768,512]{1,0:T(8,128)S(1)} fusion(f32[768,256]{1,0:T(8,128)S(1)} %add_dynamic-update-slice_fusion, f32[256,512]{1,0:T(8,128)S(1)} %copy-done.2), kind=kOutput, calls=%fused_computation.49 | convolution fusion | flops 1207959552 | bytes 2883584 | tf_op jit(solution)/shard_map/dot_general | solution.py:10
  49.9 0.1 add_add_fusion
  50.0 0.1 subtract_subtract_fusion
  50.1 0.0 copy-start.4
  50.1 0.6 fusion
  50.7 0.1 multiply_subtract_fusion
  50.8 0.1 copy-done.4
  50.9 0.4 fusion.4
  51.3 5.7 %collective-permute-start = (f32[64,256]{1,0:T(8,128)S(1)}, f32[64,256]{1,0:T(8,128)S(1)}, u32[]{:S(2)}, u32[]{:S(2)}) collective-permute-start(f32[64,256]{1,0:T(8,128)S(1)} %get-tuple-element.5), channel_id=1, source_target_pairs={{0,3},{1,2},{2,1},{3,0},{4,7},{5,6},{6,5},{7,4},{8,11},{9,10},{10,... | collective-permute-start | bytes 196616 | tf_op jit(solution)/shard_map/ppermute | solution.py:92
  57.0 3.0 %collective-permute-start.1 = (f32[64,256]{1,0:T(8,128)S(1)}, f32[64,256]{1,0:T(8,128)S(1)}, u32[]{:S(2)}, u32[]{:S(2)}) collective-permute-start(f32[64,256]{1,0:T(8,128)S(1)} %get-tuple-element.5), channel_id=1, source_target_pairs={{0,2},{1,3},{2,0},{3,1},{4,6},{5,7},{6,4},{7,5},{8,10},{9,11},{10,... | collective-permute-start | bytes 196616 | tf_op jit(solution)/shard_map/ppermute | solution.py:92
  60.0 1.9 %collective-permute-start.2 = (f32[64,256]{1,0:T(8,128)S(1)}, f32[64,256]{1,0:T(8,128)S(1)}, u32[]{:S(2)}, u32[]{:S(2)}) collective-permute-start(f32[64,256]{1,0:T(8,128)S(1)} %get-tuple-element.5), channel_id=1, source_target_pairs={{0,1},{1,0},{2,3},{3,2},{4,5},{5,4},{6,7},{7,6},{8,9},{9,8},{10,11... | collective-permute-start | bytes 196616 | tf_op jit(solution)/shard_map/ppermute | solution.py:92
  62.0 0.0 collective-permute-done
  62.0 0.8 collective-permute-done.1
  62.8 0.3 collective-permute-done.2
  63.2 0.1 all_to_all.12
  63.3 23.4 %all_to_all.18 = f32[128,1,256]{2,1,0:T(1,128)S(1)} all-to-all(f32[128,1,256]{2,1,0:T(1,128)S(1)} %all_to_all.12), channel_id=1, replica_groups=mesh['seq'=128,'batch'=4] {'seq'}, dimensions={0} | all-to-all | bytes 262144 | tf_op jit(solution)/shard_map/all_to_all | solution.py:106
  86.7 0.6 slice.189
  87.3 0.6 fusion.14
  (18 shorter events, 0.4 us)
Async XLA Ops:
  1.5 45.1 %copy-start.3 = (f32[256,64]{1,0:T(8,128)S(1)}, f32[256,64]{1,0:T(8,128)}, u32[]{:S(2)}) copy-start(f32[256,64]{1,0:T(8,128)} %constant.24.clone) | copy-start | bytes 196612
  3.6 43.8 %copy-start = (f32[128,256]{1,0:T(8,128)S(1)}, f32[128,256]{1,0:T(8,128)}, u32[]{:S(2)}) copy-start(f32[128,256]{1,0:T(8,128)} %constant.26.clone) | copy-start | bytes 393220
  3.6 43.8 %copy-start.1 = (f32[128,256]{1,0:T(8,128)S(1)}, f32[128,256]{1,0:T(8,128)}, u32[]{:S(2)}) copy-start(f32[128,256]{1,0:T(8,128)} %constant.27.clone) | copy-start | bytes 393220
  47.4 1.0 %copy-start.2 = (f32[256,512]{1,0:T(8,128)S(1)}, f32[256,512]{1,0:T(8,128)}, u32[]{:S(2)}) copy-start(f32[256,512]{1,0:T(8,128)} %constant.28.clone) | copy-start | bytes 1572868
  50.1 0.8 copy-start.4
  51.3 10.6 %collective-permute-start = (f32[64,256]{1,0:T(8,128)S(1)}, f32[64,256]{1,0:T(8,128)S(1)}, u32[]{:S(2)}, u32[]{:S(2)}) collective-permute-start(f32[64,256]{1,0:T(8,128)S(1)} %get-tuple-element.5), channel_id=1, source_target_pairs={{0,3},{1,2},{2,1},{3,0},{4,7},{5,6},{6,5},{7,4},{8,11},{9,10},{10,... | collective-permute-start | bytes 196616 | tf_op jit(solution)/shard_map/ppermute | solution.py:92
  57.0 5.8 %collective-permute-start.1 = (f32[64,256]{1,0:T(8,128)S(1)}, f32[64,256]{1,0:T(8,128)S(1)}, u32[]{:S(2)}, u32[]{:S(2)}) collective-permute-start(f32[64,256]{1,0:T(8,128)S(1)} %get-tuple-element.5), channel_id=1, source_target_pairs={{0,2},{1,3},{2,0},{3,1},{4,6},{5,7},{6,4},{7,5},{8,10},{9,11},{10,... | collective-permute-start | bytes 196616 | tf_op jit(solution)/shard_map/ppermute | solution.py:92
  60.0 3.1 %collective-permute-start.2 = (f32[64,256]{1,0:T(8,128)S(1)}, f32[64,256]{1,0:T(8,128)S(1)}, u32[]{:S(2)}, u32[]{:S(2)}) collective-permute-start(f32[64,256]{1,0:T(8,128)S(1)} %get-tuple-element.5), channel_id=1, source_target_pairs={{0,1},{1,0},{2,3},{3,2},{4,5},{5,4},{6,7},{7,6},{8,9},{9,8},{10,11... | collective-permute-start | bytes 196616 | tf_op jit(solution)/shard_map/ppermute | solution.py:92

commit v6 on v5

--- a/solution.py
+++ b/solution.py
@@ -8,7 +8,7 @@
 
 def contract(left, right):
     return jnp.matmul(
-        left, right, precision=lax.Precision.HIGHEST, preferred_element_type=jnp.float32
+        left, right, precision=lax.Precision.HIGH, preferred_element_type=jnp.float32
     )
 
 
@@ -41,8 +41,8 @@
     first, back, tw_cos, tw_sin, second = tables(outer, inner, used)
     f32 = jnp.float32
 
-    send = jnp.stack([inputs[0].astype(f32), out_grad[0].astype(f32), filters], axis=1)
-    send = send.reshape(channels, 1, 3 * length_dev)
+    send = jnp.concatenate([inputs[0], out_grad[0]], axis=1).astype(f32)
+    send = jnp.concatenate([send, filters], axis=1).reshape(channels, 1, 3 * length_dev)
     recv = lax.all_to_all(send, "seq", 0, 0, tiled=True)
     recv = recv.reshape(seq_count, 3, length_dev)
     signal = recv[:, 0].reshape(used, inner)

time: 88.6 us -> 86.4 us (0.975)
  local copies, waits for them, and re-layouts: 5.71 us -> 3.22 us
  other arithmetic: 0.6 us -> 2.26 us
  matrix products: 3.16 us -> 1.88 us
    unnamed x14 -> x11, local copies, waits for them, and re-layouts: 3.7 us -> 1.23 us
    dot_general x4, matrix products: 3.16 us -> 1.88 us  [contract(): jnp.matmul(left, right, precision=lax.Precision.HIGH, preferred_element_t...]
where the time goes in v6:
time: 86.4 us; the launch traced here: 85.8 us
  blocking collectives  65.7 us (76%)
  starting transfers between devices  10.6 us (12%)
  local copies, waits for them, and re-layouts  3.22 us (4%)
  other arithmetic  2.26 us (3%)
  matrix products  1.88 us (2%)
  waiting for transfers between devices  1.17 us (1%)
  between operations  0.95 us (1%)
    all_to_all x2, blocking collectives, body(): recv = lax.all_to_all(send, 'seq', 0, 0, tiled=True)  65.7 us
    ppermute x3, starting transfers between devices, body(): received.append(lax.ppermute(filt_row, 'batch', pairs))  10.6 us
    dot_general x4, matrix products, contract(): jnp.matmul(left, right, precision=lax.Precision.HIGH, preferred_element_t...  1.88 us
  transfers between devices with their start and end apart: 3, of which 2 were waited for; matrix products, arithmetic and copies ran while one was open for 0% of the time, Pallas kernels for 0%

profile of v6, /device:TPU:1, one launch (start us, length us, event | category | flops | bytes accessed | tf_op | source)
XLA Modules:
  0.0 85.8 jit_solution(17670000262888191438)
XLA Ops:
  0.6 0.0 copy-start.3
  0.6 0.8 maximum_convert_fusion
  1.5 0.9 %pad_maximum_fusion = f32[128,384]{1,0:T(8,128)S(1)} fusion(f32[128,128]{1,0:T(8,128)} %param.10, f32[128,256]{1,0:T(8,128)S(1)} %maximum_convert_fusion), kind=kLoop, calls=%fused_computation.8 | loop fusion | flops 49152 | bytes 393216 | tf_op jit(solution)/shard_map/concatenate | solution.py:45
  2.3 0.1 reshape.18
  2.5 0.0 copy-start
  2.5 0.0 copy-start.1
  2.5 42.4 %all_to_all.17 = f32[128,1,384]{2,1,0:T(1,128)S(1)} all-to-all(f32[128,1,384]{2,1,0:T(1,128)S(1)} %reshape.18), channel_id=1, replica_groups=mesh['seq'=128,'batch'=4] {'seq'}, dimensions={0} | all-to-all | bytes 393216 | tf_op jit(solution)/shard_map/all_to_all | solution.py:46
  44.9 0.2 copy.19
  45.1 0.1 copy.21
  45.2 0.1 copy.22
  45.3 0.1 copy.20
  45.5 0.0 copy-done.3
  45.5 0.5 fusion.8
  45.9 0.0 copy-done
  46.0 0.0 copy-done.1
  46.0 0.0 copy-start.2
  46.2 0.8 copy-done.2
  47.1 0.8 fusion.19
  47.9 0.1 add_add_fusion
  48.0 0.1 subtract_subtract_fusion
  48.1 0.0 copy-start.4
  48.1 0.4 fusion
  48.5 0.1 multiply_subtract_fusion
  48.5 0.4 copy-done.4
  48.9 0.3 fusion.4
  49.2 5.7 %collective-permute-start = (f32[64,256]{1,0:T(8,128)S(1)}, f32[64,256]{1,0:T(8,128)S(1)}, u32[]{:S(2)}, u32[]{:S(2)}) collective-permute-start(f32[64,256]{1,0:T(8,128)S(1)} %get-tuple-element.5), channel_id=1, source_target_pairs={{0,3},{1,2},{2,1},{3,0},{4,7},{5,6},{6,5},{7,4},{8,11},{9,10},{10,... | collective-permute-start | bytes 196616 | tf_op jit(solution)/shard_map/ppermute | solution.py:92
  54.9 3.0 %collective-permute-start.1 = (f32[64,256]{1,0:T(8,128)S(1)}, f32[64,256]{1,0:T(8,128)S(1)}, u32[]{:S(2)}, u32[]{:S(2)}) collective-permute-start(f32[64,256]{1,0:T(8,128)S(1)} %get-tuple-element.5), channel_id=1, source_target_pairs={{0,2},{1,3},{2,0},{3,1},{4,6},{5,7},{6,4},{7,5},{8,10},{9,11},{10,... | collective-permute-start | bytes 196616 | tf_op jit(solution)/shard_map/ppermute | solution.py:92
  57.9 1.9 %collective-permute-start.2 = (f32[64,256]{1,0:T(8,128)S(1)}, f32[64,256]{1,0:T(8,128)S(1)}, u32[]{:S(2)}, u32[]{:S(2)}) collective-permute-start(f32[64,256]{1,0:T(8,128)S(1)} %get-tuple-element.5), channel_id=1, source_target_pairs={{0,1},{1,0},{2,3},{3,2},{4,5},{5,4},{6,7},{7,6},{8,9},{9,8},{10,11... | collective-permute-start | bytes 196616 | tf_op jit(solution)/shard_map/ppermute | solution.py:92
  59.9 0.0 collective-permute-done
  59.9 0.8 collective-permute-done.1
  60.7 0.3 collective-permute-done.2
  61.1 0.1 all_to_all.12
  61.2 23.3 %all_to_all.18 = f32[128,1,256]{2,1,0:T(1,128)S(1)} all-to-all(f32[128,1,256]{2,1,0:T(1,128)S(1)} %all_to_all.12), channel_id=1, replica_groups=mesh['seq'=128,'batch'=4] {'seq'}, dimensions={0} | all-to-all | bytes 262144 | tf_op jit(solution)/shard_map/all_to_all | solution.py:106
  84.5 0.6 slice.189
  85.2 0.6 fusion.14
  (16 shorter events, 0.4 us)
Async XLA Ops:
  0.6 44.8 %copy-start.3 = (f32[256,64]{1,0:T(8,128)S(1)}, f32[256,64]{1,0:T(8,128)}, u32[]{:S(2)}) copy-start(f32[256,64]{1,0:T(8,128)} %constant.24.clone) | copy-start | bytes 196612
  2.5 43.5 %copy-start = (f32[128,256]{1,0:T(8,128)S(1)}, f32[128,256]{1,0:T(8,128)}, u32[]{:S(2)}) copy-start(f32[128,256]{1,0:T(8,128)} %constant.26.clone) | copy-start | bytes 393220
  2.5 43.5 %copy-start.1 = (f32[128,256]{1,0:T(8,128)S(1)}, f32[128,256]{1,0:T(8,128)}, u32[]{:S(2)}) copy-start(f32[128,256]{1,0:T(8,128)} %constant.27.clone) | copy-start | bytes 393220
  46.0 1.0 %copy-start.2 = (f32[256,512]{1,0:T(8,128)S(1)}, f32[256,512]{1,0:T(8,128)}, u32[]{:S(2)}) copy-start(f32[256,512]{1,0:T(8,128)} %constant.28.clone) | copy-start | bytes 1572868
  48.1 0.8 copy-start.4
  49.2 10.7 %collective-permute-start = (f32[64,256]{1,0:T(8,128)S(1)}, f32[64,256]{1,0:T(8,128)S(1)}, u32[]{:S(2)}, u32[]{:S(2)}) collective-permute-start(f32[64,256]{1,0:T(8,128)S(1)} %get-tuple-element.5), channel_id=1, source_target_pairs={{0,3},{1,2},{2,1},{3,0},{4,7},{5,6},{6,5},{7,4},{8,11},{9,10},{10,... | collective-permute-start | bytes 196616 | tf_op jit(solution)/shard_map/ppermute | solution.py:92
  54.9 5.8 %collective-permute-start.1 = (f32[64,256]{1,0:T(8,128)S(1)}, f32[64,256]{1,0:T(8,128)S(1)}, u32[]{:S(2)}, u32[]{:S(2)}) collective-permute-start(f32[64,256]{1,0:T(8,128)S(1)} %get-tuple-element.5), channel_id=1, source_target_pairs={{0,2},{1,3},{2,0},{3,1},{4,6},{5,7},{6,4},{7,5},{8,10},{9,11},{10,... | collective-permute-start | bytes 196616 | tf_op jit(solution)/shard_map/ppermute | solution.py:92
  57.9 3.1 %collective-permute-start.2 = (f32[64,256]{1,0:T(8,128)S(1)}, f32[64,256]{1,0:T(8,128)S(1)}, u32[]{:S(2)}, u32[]{:S(2)}) collective-permute-start(f32[64,256]{1,0:T(8,128)S(1)} %get-tuple-element.5), channel_id=1, source_target_pairs={{0,1},{1,0},{2,3},{3,2},{4,5},{5,4},{6,7},{7,6},{8,9},{9,8},{10,11... | collective-permute-start | bytes 196616 | tf_op jit(solution)/shard_map/ppermute | solution.py:92

commit v7 on v6

--- a/solution.py
+++ b/solution.py
@@ -86,19 +86,11 @@
     in_row = c1[:, :inner] - s1[:, inner:]
     filt_row = c1[:, inner:] + s1[:, :inner]
 
-    received = [filt_row]
-    for step in range(1, batch_count):
-        pairs = [(index, index ^ step) for index in range(batch_count)]
-        received.append(lax.ppermute(filt_row, "batch", pairs))
-    ordered = []
-    for source in range(batch_count):
-        pick = received[0]
-        for step in range(1, batch_count):
-            pick = jnp.where((mine ^ step) == source, received[step], pick)
-        ordered.append(pick)
-    filt_row = ordered[0]
+    spread = jnp.broadcast_to(filt_row[None], (batch_count,) + filt_row.shape)
+    gathered = lax.all_to_all(spread, "batch", 0, 0, tiled=True)
+    filt_row = gathered[0]
     for source in range(1, batch_count):
-        filt_row = filt_row + ordered[source]
+        filt_row = filt_row + gathered[source]
 
     send = jnp.concatenate(
         [in_row.reshape(seq_count, length_dev), filt_row.reshape(seq_count, length_dev)], axis=1

time: 86.4 us -> 87.3 us (1.010)
  waiting for transfers between devices: 1.17 us -> 5.16 us
  starting transfers between devices: 10.6 us -> 6.87 us
    ppermute x3 -> x0, starting transfers between devices: 10.6 us -> none  [body(): received.append(lax.ppermute(filt_row, 'batch', pairs))]
    all_to_all x0 -> x1, starting transfers between devices: none -> 6.87 us  [body(): gathered = lax.all_to_all(spread, 'batch', 0, 0, tiled=True)]
    all_to_all x0 -> x1, waiting for transfers between devices: none -> 5.16 us  [body(): gathered = lax.all_to_all(spread, 'batch', 0, 0, tiled=True)]
    ppermute x3 -> x0, waiting for transfers between devices: 1.17 us -> none  [body(): received.append(lax.ppermute(filt_row, 'batch', pairs))]
  transfers between devices with their start and end apart: 3 -> 1, of which waited for: 2 -> 1; matrix products, arithmetic and copies ran while one was open for 0% -> 0% of each run, Pallas kernels for 0% -> 0%
where the time goes in v7:
time: 87.3 us; the launch traced here: 85.9 us
  blocking collectives  65 us (74%)
  starting transfers between devices  6.87 us (8%)
  waiting for transfers between devices  5.16 us (6%)
  local copies, waits for them, and re-layouts  3.94 us (5%)
  other arithmetic  2.23 us (3%)
  matrix products  1.88 us (2%)
  between operations  0.88 us (1%)
    all_to_all x2, blocking collectives, body(): recv = lax.all_to_all(send, 'seq', 0, 0, tiled=True)  65 us
    all_to_all x1, starting transfers between devices, body(): gathered = lax.all_to_all(spread, 'batch', 0, 0, tiled=True)  6.87 us
    all_to_all x1, waiting for transfers between devices, body(): gathered = lax.all_to_all(spread, 'batch', 0, 0, tiled=True)  5.16 us
    dot_general x4, matrix products, contract(): jnp.matmul(left, right, precision=lax.Precision.HIGH, preferred_element_t...  1.88 us
  transfers between devices with their start and end apart: 1, of which 1 were waited for; matrix products, arithmetic and copies ran while one was open for 0% of the time, Pallas kernels for 0%

profile of v7, /device:TPU:1, one launch (start us, length us, event | category | flops | bytes accessed | tf_op | source)
XLA Modules:
  0.0 85.9 jit_solution(6817233976961207562)
XLA Ops:
  0.6 0.0 copy-start.3
  0.6 0.8 maximum_convert_fusion
  1.5 0.9 pad_maximum_fusion
  2.3 0.1 reshape.24
  2.5 0.0 copy-start
  2.5 0.0 copy-start.1
  2.5 42.4 %all_to_all.22 = f32[128,1,384]{2,1,0:T(1,128)S(1)} all-to-all(f32[128,1,384]{2,1,0:T(1,128)S(1)} %reshape.24), channel_id=1, replica_groups=mesh['seq'=128,'batch'=4] {'seq'}, dimensions={0} | all-to-all | bytes 393216 | tf_op jit(solution)/shard_map/all_to_all | solution.py:46
  44.9 0.2 copy.19
  45.1 0.1 copy.20
  45.2 0.1 copy.22
  45.3 0.1 copy.21
  45.5 0.0 copy-done.3
  45.5 0.5 fusion.8
  45.9 0.0 copy-done
  46.0 0.0 copy-done.1
  46.0 0.0 copy-start.2
  46.2 0.8 copy-done.2
  47.1 0.8 fusion.19
  47.9 0.1 subtract_subtract_fusion
  48.0 0.1 add_add_fusion
  48.1 0.0 copy-start.4
  48.1 0.4 fusion
  48.5 0.1 multiply_subtract_fusion
  48.5 0.4 copy-done.4
  48.9 0.3 fusion.4
  49.2 0.7 broadcast_in_dim.4
  49.9 6.9 %all-to-all-start.1 = ((f32[4,64,256]{2,1,0:T(8,128)}), f32[4,64,256]{2,1,0:T(8,128)S(1)}, u32[]{:S(2)}, u32[]{:S(2)}) async-start(f32[4,64,256]{2,1,0:T(8,128)} %broadcast_in_dim.4), calls=%async_computation.1 | async-start | bytes 524288 | tf_op jit(solution)/shard_map/all_to_all | solution.py:90
  56.8 5.2 %all-to-all-done.1 = f32[4,64,256]{2,1,0:T(8,128)S(1)} async-done(((f32[4,64,256]{2,1,0:T(8,128)}), f32[4,64,256]{2,1,0:T(8,128)S(1)}, u32[]{:S(2)}, u32[]{:S(2)}) %all-to-all-start.1) | async-done | bytes 262176 | tf_op jit(solution)/shard_map/all_to_all | solution.py:90
  62.0 0.1 all_to_all.16
  62.1 22.6 %all_to_all.23 = f32[128,1,256]{2,1,0:T(1,128)S(1)} all-to-all(f32[128,1,256]{2,1,0:T(1,128)S(1)} %all_to_all.16), channel_id=1, replica_groups=mesh['seq'=128,'batch'=4] {'seq'}, dimensions={0} | all-to-all | bytes 262144 | tf_op jit(solution)/shard_map/all_to_all | solution.py:98
  84.7 0.6 fusion.14
  85.3 0.6 slice.209
  (16 shorter events, 0.4 us)
Async XLA Ops:
  0.6 44.8 %copy-start.3 = (f32[256,64]{1,0:T(8,128)S(1)}, f32[256,64]{1,0:T(8,128)}, u32[]{:S(2)}) copy-start(f32[256,64]{1,0:T(8,128)} %constant.12.clone) | copy-start | bytes 196612
  2.5 43.5 %copy-start = (f32[128,256]{1,0:T(8,128)S(1)}, f32[128,256]{1,0:T(8,128)}, u32[]{:S(2)}) copy-start(f32[128,256]{1,0:T(8,128)} %constant.15.clone) | copy-start | bytes 393220
  2.5 43.5 %copy-start.1 = (f32[128,256]{1,0:T(8,128)S(1)}, f32[128,256]{1,0:T(8,128)}, u32[]{:S(2)}) copy-start(f32[128,256]{1,0:T(8,128)} %constant.14.clone) | copy-start | bytes 393220
  46.0 1.0 %copy-start.2 = (f32[256,512]{1,0:T(8,128)S(1)}, f32[256,512]{1,0:T(8,128)}, u32[]{:S(2)}) copy-start(f32[256,512]{1,0:T(8,128)} %constant.16.clone) | copy-start | bytes 1572868
  48.1 0.8 copy-start.4
  49.9 12.0 %all-to-all-start.1 = ((f32[4,64,256]{2,1,0:T(8,128)}), f32[4,64,256]{2,1,0:T(8,128)S(1)}, u32[]{:S(2)}, u32[]{:S(2)}) async-start(f32[4,64,256]{2,1,0:T(8,128)} %broadcast_in_dim.4), calls=%async_computation.1 | async-start | bytes 524288 | tf_op jit(solution)/shard_map/all_to_all | solution.py:90

commit v8 on v7

--- a/solution.py
+++ b/solution.py
@@ -3,7 +3,7 @@
 import jax
 import jax.numpy as jnp
 from jax import lax
-from jax.sharding import PartitionSpec as P
+from jax.sharding import Mesh, PartitionSpec as P
 
 
 def contract(left, right):
@@ -28,8 +28,6 @@
 
 def body(inputs, out_grad, filters):
     seq_count = lax.axis_size("seq")
-    batch_count = lax.axis_size("batch")
-    mine = lax.axis_index("batch")
     channels = inputs.shape[1]
     length_dev = inputs.shape[2]
     assert channels == seq_count and inputs.shape[0] == 1
@@ -86,27 +84,44 @@
     in_row = c1[:, :inner] - s1[:, inner:]
     filt_row = c1[:, inner:] + s1[:, :inner]
 
-    spread = jnp.broadcast_to(filt_row[None], (batch_count,) + filt_row.shape)
-    gathered = lax.all_to_all(spread, "batch", 0, 0, tiled=True)
-    filt_row = gathered[0]
-    for source in range(1, batch_count):
-        filt_row = filt_row + gathered[source]
+    cores = lax.axis_size("core")
+    pairs = [(index, index ^ 1) for index in range(cores)]
+    filt_row = filt_row + lax.ppermute(filt_row, "core", pairs)
 
+    rows_count = lax.axis_size("rows")
+    row = lax.axis_index("rows")
+    own = (jnp.arange(rows_count) == row)[None, :, None]
+    in_blocks = in_row.reshape(seq_count, length_dev)
+    filt_blocks = filt_row.reshape(seq_count, length_dev)
     send = jnp.concatenate(
-        [in_row.reshape(seq_count, length_dev), filt_row.reshape(seq_count, length_dev)], axis=1
-    )
-    recv = lax.all_to_all(send, "seq", 0, 0, tiled=True)
-    in_grad = recv[:, :length_dev]
-    filter_grad = recv[:, length_dev:]
+        [
+            jnp.where(own, in_blocks[:, None, :], 0.0),
+            jnp.broadcast_to(filt_blocks[:, None, :], (seq_count, rows_count, length_dev)),
+        ],
+        axis=2,
+    ).reshape(seq_count * rows_count, 1, 2 * length_dev)
+    recv = lax.all_to_all(send, ("seq", "rows"), 0, 0, tiled=True)
+    recv = recv.reshape(seq_count, rows_count, 2 * length_dev)
+    in_grad = lax.dynamic_index_in_dim(recv[:, :, :length_dev], row, axis=1, keepdims=False)
+    parts = recv[:, :, length_dev:]
+    filter_grad = parts[:, 0]
+    for index in range(1, rows_count):
+        filter_grad = filter_grad + parts[:, index]
     return (in_grad.astype(jnp.bfloat16)[None], filter_grad)
 
 
 def solution(mesh):
-    placed = (P("batch", None, "seq"), P("batch", None, "seq"), P(None, "seq"))
+    seq_count, batch_count = mesh.devices.shape
+    cores = 2
+    split = Mesh(
+        mesh.devices.reshape(seq_count, batch_count // cores, cores), ("seq", "rows", "core")
+    )
+    batch = ("rows", "core")
+    placed = (P(batch, None, "seq"), P(batch, None, "seq"), P(None, "seq"))
     return jax.shard_map(
         body,
-        mesh=mesh,
+        mesh=split,
         in_specs=placed,
-        out_specs=(P("batch", None, "seq"), P(None, "seq")),
+        out_specs=(P(batch, None, "seq"), P(None, "seq")),
         check_vma=False,
     )

time: 87.3 us -> 92.9 us (1.064)
  blocking collectives: 65 us -> 0 us
  waiting for transfers between devices: 5.16 us -> 43.7 us
  starting transfers between devices: 6.87 us -> 37.5 us
  other arithmetic: 2.23 us -> 4.82 us
    all_to_all x2 -> x0, blocking collectives: 65 us -> none  [body(): recv = lax.all_to_all(send, 'seq', 0, 0, tiled=True)]
    all_to_all x1 -> x2, waiting for transfers between devices: 5.16 us -> 43.2 us  [the longest x1 23.7 us: body(): recv = lax.all_to_all(send, ('seq', 'rows'), 0, 0, tiled=True)]
    all_to_all x1 -> x2, starting transfers between devices: 6.87 us -> 32.2 us  [the longest x1 23.1 us: body(): recv = lax.all_to_all(send, 'seq', 0, 0, tiled=True)]
    ppermute x0 -> x1, starting transfers between devices: none -> 5.25 us  [body(): filt_row = filt_row + lax.ppermute(filt_row, 'core', pairs)]
    broadcast_in_dim x2 -> x6, local copies, waits for them, and re-layouts: 1.34 us -> 0.26 us  [the longest x4 0.21 us: body(): jnp.where(own, in_blocks[:, None, :], 0.0)]
    concatenate x1, other arithmetic: 0.01 us -> 0.95 us  [body(): jnp.concatenate([jnp.where(own, in_blocks[:, None, :], 0.0), jnp.broadcas...]
  transfers between devices with their start and end apart: 1 -> 3, of which waited for: 1 -> 3; matrix products, arithmetic and copies ran while one was open for 0% -> 1% of each run, Pallas kernels for 0% -> 0%
where the time goes in v8:
time: 92.9 us; the launch traced here: 92.5 us
  waiting for transfers between devices  43.7 us (47%)
  starting transfers between devices  37.5 us (40%)
  other arithmetic  4.82 us (5%)
  local copies, waits for them, and re-layouts  3.67 us (4%)
  matrix products  1.88 us (2%)
  between operations  0.93 us (1%)
    all_to_all x1, waiting for transfers between devices, body(): recv = lax.all_to_all(send, ('seq', 'rows'), 0, 0, tiled=True)  23.7 us
    all_to_all x1, starting transfers between devices, body(): recv = lax.all_to_all(send, 'seq', 0, 0, tiled=True)  23.1 us
    all_to_all x1, waiting for transfers between devices, body(): recv = lax.all_to_all(send, 'seq', 0, 0, tiled=True)  19.5 us
    all_to_all x1, starting transfers between devices, body(): recv = lax.all_to_all(send, ('seq', 'rows'), 0, 0, tiled=True)  9.13 us
    ppermute x1, starting transfers between devices, body(): filt_row = filt_row + lax.ppermute(filt_row, 'core', pairs)  5.25 us
    dot_general x4, matrix products, contract(): jnp.matmul(left, right, precision=lax.Precision.HIGH, preferred_element_t...  1.88 us
  transfers between devices with their start and end apart: 3, of which 3 were waited for; matrix products, arithmetic and copies ran while one was open for 1% of the time, Pallas kernels for 0%

profile of v8, /device:TPU:1, one launch (start us, length us, event | category | flops | bytes accessed | tf_op | source)
XLA Modules:
  0.0 92.5 jit_solution(6582342524916061609)
XLA Ops:
  0.6 0.0 copy-start.3
  0.6 0.8 maximum_convert_fusion
  1.5 0.9 pad_maximum_fusion.1
  2.3 0.8 reshape.68
  3.1 0.0 copy-start
  3.1 0.0 copy-start.1
  3.1 23.1 %all-to-all-start = ((f32[128,1,384]{2,1,0:T(1,128)}), f32[128,1,384]{2,1,0:T(1,128)S(1)}, u32[]{:S(2)}, u32[]{:S(2)}) async-start(f32[128,1,384]{2,1,0:T(1,128)} %reshape.68), calls=%async_computation | async-start | bytes 393216 | tf_op jit(solution)/shard_map/all_to_all | solution.py:44
  26.3 0.1 broadcast_in_dim.38
  26.4 19.5 %all-to-all-done = f32[128,1,384]{2,1,0:T(1,128)S(1)} async-done(((f32[128,1,384]{2,1,0:T(1,128)}), f32[128,1,384]{2,1,0:T(1,128)S(1)}, u32[]{:S(2)}, u32[]{:S(2)}) %all-to-all-start) | async-done | bytes 196640 | tf_op jit(solution)/shard_map/all_to_all | solution.py:44
  45.9 0.2 copy.19
  46.1 0.1 copy.21
  46.2 0.1 copy.22
  46.3 0.1 copy.20
  46.5 0.0 copy-done.3
  46.5 0.5 fusion.8
  46.9 0.0 copy-done
  46.9 0.0 copy-done.1
  47.0 0.0 copy-start.2
  47.2 0.8 copy-done.2
  48.0 0.8 fusion.18
  48.8 0.1 add_add_fusion
  49.0 0.1 subtract_subtract_fusion
  49.1 0.0 copy-start.4
  49.1 0.4 fusion
  49.5 0.1 multiply_subtract_fusion
  49.5 0.4 copy-done.4
  49.9 0.3 fusion.4
  50.2 5.3 %collective-permute-start = (f32[64,256]{1,0:T(8,128)S(1)}, f32[64,256]{1,0:T(8,128)S(1)}, u32[]{:S(2)}, u32[]{:S(2)}) collective-permute-start(f32[64,256]{1,0:T(8,128)S(1)} %get-tuple-element.5), channel_id=1, source_target_pairs={{0,1},{1,0},{2,3},{3,2},{4,5},{5,4},{6,7},{7,6},{8,9},{9,8},{10,11... | collective-permute-start | bytes 196616 | tf_op jit(solution)/shard_map/ppermute | solution.py:89
  55.5 0.3 broadcast_select_fusion
  55.9 0.5 collective-permute-done
  56.4 0.9 %pad_maximum_fusion = f32[256,1,256]{2,1,0:T(1,128)} fusion(f32[256,1,128]{2,1,0:T(1,128)S(1)} %bitcast.22, f32[256,1,128]{2,1,0:T(1,128)S(1)} %broadcast_select_fusion), kind=kLoop, calls=%fused_computation.8 | loop fusion | flops 65536 | bytes 524288 | tf_op jit(solution)/shard_map/concatenate | solution.py:96
  57.4 9.1 %all-to-all-start.1 = ((f32[256,1,256]{2,1,0:T(1,128)}), f32[256,1,256]{2,1,0:T(1,128)S(1)}, u32[]{:S(2)}, u32[]{:S(2)}) async-start(f32[256,1,256]{2,1,0:T(1,128)} %pad_maximum_fusion), calls=%async_computation.1 | async-start | bytes 524288 | tf_op jit(solution)/shard_map/all_to_all | solution.py:103
  66.5 23.7 %all-to-all-done.1 = f32[256,1,256]{2,1,0:T(1,128)S(1)} async-done(((f32[256,1,256]{2,1,0:T(1,128)}), f32[256,1,256]{2,1,0:T(1,128)S(1)}, u32[]{:S(2)}, u32[]{:S(2)}) %all-to-all-start.1) | async-done | bytes 262176 | tf_op jit(solution)/shard_map/all_to_all | solution.py:103
  90.2 0.6 reduce
  90.9 0.1 reshape.70
  91.1 0.7 slice_add_fusion.4
  91.8 0.1 dynamic-slice_convert_fusion
  91.8 0.6 copy.26
  (19 shorter events, 0.5 us)
Async XLA Ops:
  0.6 45.8 %copy-start.3 = (f32[256,64]{1,0:T(8,128)S(1)}, f32[256,64]{1,0:T(8,128)}, u32[]{:S(2)}) copy-start(f32[256,64]{1,0:T(8,128)} %constant.24.clone) | copy-start | bytes 196612
  3.1 43.8 %copy-start = (f32[128,256]{1,0:T(8,128)S(1)}, f32[128,256]{1,0:T(8,128)}, u32[]{:S(2)}) copy-start(f32[128,256]{1,0:T(8,128)} %constant.26.clone) | copy-start | bytes 393220
  3.1 43.8 %copy-start.1 = (f32[128,256]{1,0:T(8,128)S(1)}, f32[128,256]{1,0:T(8,128)}, u32[]{:S(2)}) copy-start(f32[128,256]{1,0:T(8,128)} %constant.27.clone) | copy-start | bytes 393220
  3.1 42.8 %all-to-all-start = ((f32[128,1,384]{2,1,0:T(1,128)}), f32[128,1,384]{2,1,0:T(1,128)S(1)}, u32[]{:S(2)}, u32[]{:S(2)}) async-start(f32[128,1,384]{2,1,0:T(1,128)} %reshape.68), calls=%async_computation | async-start | bytes 393216 | tf_op jit(solution)/shard_map/all_to_all | solution.py:44
  47.0 1.0 %copy-start.2 = (f32[256,512]{1,0:T(8,128)S(1)}, f32[256,512]{1,0:T(8,128)}, u32[]{:S(2)}) copy-start(f32[256,512]{1,0:T(8,128)} %constant.28.clone) | copy-start | bytes 1572868
  49.1 0.8 copy-start.4
  50.2 6.1 %collective-permute-start = (f32[64,256]{1,0:T(8,128)S(1)}, f32[64,256]{1,0:T(8,128)S(1)}, u32[]{:S(2)}, u32[]{:S(2)}) collective-permute-start(f32[64,256]{1,0:T(8,128)S(1)} %get-tuple-element.5), channel_id=1, source_target_pairs={{0,1},{1,0},{2,3},{3,2},{4,5},{5,4},{6,7},{7,6},{8,9},{9,8},{10,11... | collective-permute-start | bytes 196616 | tf_op jit(solution)/shard_map/ppermute | solution.py:89
  57.4 32.9 %all-to-all-start.1 = ((f32[256,1,256]{2,1,0:T(1,128)}), f32[256,1,256]{2,1,0:T(1,128)S(1)}, u32[]{:S(2)}, u32[]{:S(2)}) async-start(f32[256,1,256]{2,1,0:T(1,128)} %pad_maximum_fusion), calls=%async_computation.1 | async-start | bytes 524288 | tf_op jit(solution)/shard_map/all_to_all | solution.py:103

commit v9 on v6

--- a/solution.py
+++ b/solution.py
@@ -22,8 +22,13 @@
     k2 = np.arange(inner)
     theta2 = 2.0 * np.pi * np.outer(k2, k2) / inner
     second = np.concatenate([np.cos(theta2), np.sin(theta2)], axis=1)
-    as32 = lambda a: jnp.asarray(a.astype(np.float32))
-    return as32(first), as32(back), as32(np.cos(phi)), as32(np.sin(phi)), as32(second)
+    width = second.shape[1]
+    pad = lambda a: np.pad(a, ((0, 0), (0, width - a.shape[1])))
+    pieces = [second, pad(first), pad(back), pad(np.cos(phi)), pad(np.sin(phi))]
+    starts = np.cumsum([0] + [piece.shape[0] for piece in pieces])
+    packed = lax.optimization_barrier(jnp.asarray(np.concatenate(pieces).astype(np.float32)))
+    cut = lambda i, cols: packed[starts[i] : starts[i + 1], :cols]
+    return cut(1, used), cut(2, outer), cut(3, inner), cut(4, inner), cut(0, width)
 
 
 def body(inputs, out_grad, filters):

time: 86.4 us -> 86 us (level)
  blocking collectives: 65.7 us -> 23.3 us
  starting transfers between devices: 10.6 us -> 33.4 us
  waiting for transfers between devices: 1.17 us -> 20.8 us
    all_to_all x2 -> x1, blocking collectives: 65.7 us -> 23.3 us  [body(): recv = lax.all_to_all(send, 'seq', 0, 0, tiled=True)]
    all_to_all x0 -> x1, starting transfers between devices: none -> 23 us  [body(): recv = lax.all_to_all(send, 'seq', 0, 0, tiled=True)]
    all_to_all x0 -> x1, waiting for transfers between devices: none -> 19.7 us  [body(): recv = lax.all_to_all(send, 'seq', 0, 0, tiled=True)]
    unnamed x11 -> x3, local copies, waits for them, and re-layouts: 1.23 us -> 0.02 us
  transfers between devices with their start and end apart: 3 -> 4, of which waited for: 2 -> 3; matrix products, arithmetic and copies ran while one was open for 0% -> 0% of each run, Pallas kernels for 0% -> 0%
where the time goes in v9:
time: 86 us; the launch traced here: 85.4 us
  starting transfers between devices  33.4 us (39%)
  blocking collectives  23.3 us (27%)
  waiting for transfers between devices  20.8 us (24%)
  local copies, waits for them, and re-layouts  2.68 us (3%)
  other arithmetic  2.42 us (3%)
  matrix products  1.9 us (2%)
  between operations  0.89 us (1%)
    all_to_all x1, blocking collectives, body(): recv = lax.all_to_all(send, 'seq', 0, 0, tiled=True)  23.3 us
    all_to_all x1, starting transfers between devices, body(): recv = lax.all_to_all(send, 'seq', 0, 0, tiled=True)  23 us
    all_to_all x1, waiting for transfers between devices, body(): recv = lax.all_to_all(send, 'seq', 0, 0, tiled=True)  19.7 us
    ppermute x3, starting transfers between devices, body(): received.append(lax.ppermute(filt_row, 'batch', pairs))  10.4 us
    dot_general x4, matrix products, contract(): jnp.matmul(left, right, precision=lax.Precision.HIGH, preferred_element_t...  1.9 us
  transfers between devices with their start and end apart: 4, of which 3 were waited for; matrix products, arithmetic and copies ran while one was open for 0% of the time, Pallas kernels for 0%

profile of v9, /device:TPU:1, one launch (start us, length us, event | category | flops | bytes accessed | tf_op | source)
XLA Modules:
  0.0 85.4 jit_solution(1330469972744385462)
XLA Ops:
  0.6 0.0 copy-start
  0.6 0.9 %maximum_convert_fusion = f32[128,256]{1,0:T(8,128)S(1)} fusion(bf16[128,128]{1,0:T(8,128)(2,1)} %bitcast.18, bf16[128,128]{1,0:T(8,128)(2,1)} %bitcast.19), kind=kLoop, calls=%fused_computation.46 | loop fusion | flops 131072 | bytes 196608 | tf_op jit(solution)/shard_map/convert_element_type | solution.py:49
  1.6 0.9 %pad_maximum_fusion = f32[128,384]{1,0:T(8,128)S(1)} fusion(f32[128,128]{1,0:T(8,128)} %param.6, f32[128,256]{1,0:T(8,128)S(1)} %maximum_convert_fusion), kind=kLoop, calls=%fused_computation.11 | loop fusion | flops 49152 | bytes 393216 | tf_op jit(solution)/shard_map/concatenate | solution.py:50
  2.4 0.8 reshape.18
  3.2 23.0 %all-to-all-start = ((f32[128,1,384]{2,1,0:T(1,128)}), f32[128,1,384]{2,1,0:T(1,128)S(1)}, u32[]{:S(2)}, u32[]{:S(2)}) async-start(f32[128,1,384]{2,1,0:T(1,128)} %reshape.18), calls=%async_computation | async-start | bytes 393216 | tf_op jit(solution)/shard_map/all_to_all | solution.py:51
  26.2 19.7 %all-to-all-done = f32[128,1,384]{2,1,0:T(1,128)S(1)} async-done(((f32[128,1,384]{2,1,0:T(1,128)}), f32[128,1,384]{2,1,0:T(1,128)S(1)}, u32[]{:S(2)}, u32[]{:S(2)}) %all-to-all-start) | async-done | bytes 196640 | tf_op jit(solution)/shard_map/all_to_all | solution.py:51
  45.9 0.2 copy.15
  46.0 0.1 copy.17
  46.2 0.1 copy.18
  46.3 0.1 copy.16
  46.4 0.0 copy-done
  46.4 0.5 fusion.11
  47.0 0.1 subtract_dynamic-update-slice_fusion.1
  47.1 0.1 add_dynamic-update-slice_fusion.1
  47.2 0.8 fusion.2
  48.0 0.1 add_add_fusion
  48.1 0.1 subtract_subtract_fusion
  48.2 0.4 fusion
  48.6 0.1 multiply_subtract_fusion
  48.7 0.3 fusion.7
  49.0 5.5 %collective-permute-start = (f32[64,256]{1,0:T(8,128)S(1)}, f32[64,256]{1,0:T(8,128)S(1)}, u32[]{:S(2)}, u32[]{:S(2)}) collective-permute-start(f32[64,256]{1,0:T(8,128)S(1)} %get-tuple-element.5), channel_id=1, source_target_pairs={{0,3},{1,2},{2,1},{3,0},{4,7},{5,6},{6,5},{7,4},{8,11},{9,10},{10,... | collective-permute-start | bytes 196616 | tf_op jit(solution)/shard_map/ppermute | solution.py:97
  54.5 3.0 %collective-permute-start.1 = (f32[64,256]{1,0:T(8,128)S(1)}, f32[64,256]{1,0:T(8,128)S(1)}, u32[]{:S(2)}, u32[]{:S(2)}) collective-permute-start(f32[64,256]{1,0:T(8,128)S(1)} %get-tuple-element.5), channel_id=1, source_target_pairs={{0,2},{1,3},{2,0},{3,1},{4,6},{5,7},{6,4},{7,5},{8,10},{9,11},{10,... | collective-permute-start | bytes 196616 | tf_op jit(solution)/shard_map/ppermute | solution.py:97
  57.5 1.9 %collective-permute-start.2 = (f32[64,256]{1,0:T(8,128)S(1)}, f32[64,256]{1,0:T(8,128)S(1)}, u32[]{:S(2)}, u32[]{:S(2)}) collective-permute-start(f32[64,256]{1,0:T(8,128)S(1)} %get-tuple-element.5), channel_id=1, source_target_pairs={{0,1},{1,0},{2,3},{3,2},{4,5},{5,4},{6,7},{7,6},{8,9},{9,8},{10,11... | collective-permute-start | bytes 196616 | tf_op jit(solution)/shard_map/ppermute | solution.py:97
  59.5 0.0 collective-permute-done
  59.5 0.8 collective-permute-done.1
  60.3 0.3 collective-permute-done.2
  60.7 0.1 all_to_all.12
  60.8 23.3 %all_to_all.17 = f32[128,1,256]{2,1,0:T(1,128)S(1)} all-to-all(f32[128,1,256]{2,1,0:T(1,128)S(1)} %all_to_all.12), channel_id=1, replica_groups=mesh['seq'=128,'batch'=4] {'seq'}, dimensions={0} | all-to-all | bytes 262144 | tf_op jit(solution)/shard_map/all_to_all | solution.py:111
  84.2 0.6 slice.214
  84.8 0.6 fusion.19
  (14 shorter events, 0.4 us)
Async XLA Ops:
  0.6 45.8 %copy-start = (f32[896,512]{1,0:T(8,128)S(1)}, f32[896,512]{1,0:T(8,128)}, u32[]{:S(2)}) copy-start(f32[896,512]{1,0:T(8,128)} %constant.16.clone) | copy-start | bytes 5505028
  3.2 42.6 %all-to-all-start = ((f32[128,1,384]{2,1,0:T(1,128)}), f32[128,1,384]{2,1,0:T(1,128)S(1)}, u32[]{:S(2)}, u32[]{:S(2)}) async-start(f32[128,1,384]{2,1,0:T(1,128)} %reshape.18), calls=%async_computation | async-start | bytes 393216 | tf_op jit(solution)/shard_map/all_to_all | solution.py:51
  49.0 10.5 %collective-permute-start = (f32[64,256]{1,0:T(8,128)S(1)}, f32[64,256]{1,0:T(8,128)S(1)}, u32[]{:S(2)}, u32[]{:S(2)}) collective-permute-start(f32[64,256]{1,0:T(8,128)S(1)} %get-tuple-element.5), channel_id=1, source_target_pairs={{0,3},{1,2},{2,1},{3,0},{4,7},{5,6},{6,5},{7,4},{8,11},{9,10},{10,... | collective-permute-start | bytes 196616 | tf_op jit(solution)/shard_map/ppermute | solution.py:97
  54.5 5.8 %collective-permute-start.1 = (f32[64,256]{1,0:T(8,128)S(1)}, f32[64,256]{1,0:T(8,128)S(1)}, u32[]{:S(2)}, u32[]{:S(2)}) collective-permute-start(f32[64,256]{1,0:T(8,128)S(1)} %get-tuple-element.5), channel_id=1, source_target_pairs={{0,2},{1,3},{2,0},{3,1},{4,6},{5,7},{6,4},{7,5},{8,10},{9,11},{10,... | collective-permute-start | bytes 196616 | tf_op jit(solution)/shard_map/ppermute | solution.py:97
  57.5 3.1 %collective-permute-start.2 = (f32[64,256]{1,0:T(8,128)S(1)}, f32[64,256]{1,0:T(8,128)S(1)}, u32[]{:S(2)}, u32[]{:S(2)}) collective-permute-start(f32[64,256]{1,0:T(8,128)S(1)} %get-tuple-element.5), channel_id=1, source_target_pairs={{0,1},{1,0},{2,3},{3,2},{4,5},{5,4},{6,7},{7,6},{8,9},{9,8},{10,11... | collective-permute-start | bytes 196616 | tf_op jit(solution)/shard_map/ppermute | solution.py:97

commit v10 on v9

--- a/solution.py
+++ b/solution.py
@@ -91,10 +91,10 @@
     in_row = c1[:, :inner] - s1[:, inner:]
     filt_row = c1[:, inner:] + s1[:, :inner]
 
-    received = [filt_row]
-    for step in range(1, batch_count):
+    received = [filt_row] + [None] * (batch_count - 1)
+    for step in reversed(range(1, batch_count)):
         pairs = [(index, index ^ step) for index in range(batch_count)]
-        received.append(lax.ppermute(filt_row, "batch", pairs))
+        received[step] = lax.ppermute(filt_row, "batch", pairs)
     ordered = []
     for source in range(batch_count):
         pick = received[0]

time: 86 us -> 86 us (level)
  no operation moved by 1% of the time
where the time goes in v10:
time: 86 us; the launch traced here: 85.4 us
  starting transfers between devices  33.4 us (39%)
  blocking collectives  23.3 us (27%)
  waiting for transfers between devices  20.8 us (24%)
  local copies, waits for them, and re-layouts  2.68 us (3%)
  other arithmetic  2.42 us (3%)
  matrix products  1.9 us (2%)
  between operations  0.89 us (1%)
    all_to_all x1, blocking collectives, body(): recv = lax.all_to_all(send, 'seq', 0, 0, tiled=True)  23.3 us
    all_to_all x1, starting transfers between devices, body(): recv = lax.all_to_all(send, 'seq', 0, 0, tiled=True)  23 us
    all_to_all x1, waiting for transfers between devices, body(): recv = lax.all_to_all(send, 'seq', 0, 0, tiled=True)  19.7 us
    ppermute x3, starting transfers between devices, body(): received[step] = lax.ppermute(filt_row, 'batch', pairs)  10.4 us
    dot_general x4, matrix products, contract(): jnp.matmul(left, right, precision=lax.Precision.HIGH, preferred_element_t...  1.9 us
  transfers between devices with their start and end apart: 4, of which 3 were waited for; matrix products, arithmetic and copies ran while one was open for 0% of the time, Pallas kernels for 0%

profile of v10, /device:TPU:1, one launch (start us, length us, event | category | flops | bytes accessed | tf_op | source)
XLA Modules:
  0.0 85.4 jit_solution(1330469972744385462)
XLA Ops:
  0.6 0.0 copy-start
  0.6 0.9 %maximum_convert_fusion = f32[128,256]{1,0:T(8,128)S(1)} fusion(bf16[128,128]{1,0:T(8,128)(2,1)} %bitcast.18, bf16[128,128]{1,0:T(8,128)(2,1)} %bitcast.19), kind=kLoop, calls=%fused_computation.46 | loop fusion | flops 131072 | bytes 196608 | tf_op jit(solution)/shard_map/convert_element_type | solution.py:49
  1.6 0.9 %pad_maximum_fusion = f32[128,384]{1,0:T(8,128)S(1)} fusion(f32[128,128]{1,0:T(8,128)} %param.6, f32[128,256]{1,0:T(8,128)S(1)} %maximum_convert_fusion), kind=kLoop, calls=%fused_computation.11 | loop fusion | flops 49152 | bytes 393216 | tf_op jit(solution)/shard_map/concatenate | solution.py:50
  2.4 0.8 reshape.18
  3.2 23.0 %all-to-all-start = ((f32[128,1,384]{2,1,0:T(1,128)}), f32[128,1,384]{2,1,0:T(1,128)S(1)}, u32[]{:S(2)}, u32[]{:S(2)}) async-start(f32[128,1,384]{2,1,0:T(1,128)} %reshape.18), calls=%async_computation | async-start | bytes 393216 | tf_op jit(solution)/shard_map/all_to_all | solution.py:51
  26.2 19.7 %all-to-all-done = f32[128,1,384]{2,1,0:T(1,128)S(1)} async-done(((f32[128,1,384]{2,1,0:T(1,128)}), f32[128,1,384]{2,1,0:T(1,128)S(1)}, u32[]{:S(2)}, u32[]{:S(2)}) %all-to-all-start) | async-done | bytes 196640 | tf_op jit(solution)/shard_map/all_to_all | solution.py:51
  45.9 0.2 copy.15
  46.0 0.1 copy.17
  46.2 0.1 copy.18
  46.3 0.1 copy.16
  46.4 0.0 copy-done
  46.4 0.5 fusion.11
  47.0 0.1 subtract_dynamic-update-slice_fusion.1
  47.1 0.1 add_dynamic-update-slice_fusion.1
  47.2 0.8 fusion.2
  48.0 0.1 add_add_fusion
  48.1 0.1 subtract_subtract_fusion
  48.2 0.4 fusion
  48.6 0.1 multiply_subtract_fusion
  48.7 0.3 fusion.7
  49.0 5.5 %collective-permute-start = (f32[64,256]{1,0:T(8,128)S(1)}, f32[64,256]{1,0:T(8,128)S(1)}, u32[]{:S(2)}, u32[]{:S(2)}) collective-permute-start(f32[64,256]{1,0:T(8,128)S(1)} %get-tuple-element.5), channel_id=1, source_target_pairs={{0,3},{1,2},{2,1},{3,0},{4,7},{5,6},{6,5},{7,4},{8,11},{9,10},{10,... | collective-permute-start | bytes 196616 | tf_op jit(solution)/shard_map/ppermute | solution.py:97
  54.5 3.0 %collective-permute-start.1 = (f32[64,256]{1,0:T(8,128)S(1)}, f32[64,256]{1,0:T(8,128)S(1)}, u32[]{:S(2)}, u32[]{:S(2)}) collective-permute-start(f32[64,256]{1,0:T(8,128)S(1)} %get-tuple-element.5), channel_id=1, source_target_pairs={{0,2},{1,3},{2,0},{3,1},{4,6},{5,7},{6,4},{7,5},{8,10},{9,11},{10,... | collective-permute-start | bytes 196616 | tf_op jit(solution)/shard_map/ppermute | solution.py:97
  57.5 1.9 %collective-permute-start.2 = (f32[64,256]{1,0:T(8,128)S(1)}, f32[64,256]{1,0:T(8,128)S(1)}, u32[]{:S(2)}, u32[]{:S(2)}) collective-permute-start(f32[64,256]{1,0:T(8,128)S(1)} %get-tuple-element.5), channel_id=1, source_target_pairs={{0,1},{1,0},{2,3},{3,2},{4,5},{5,4},{6,7},{7,6},{8,9},{9,8},{10,11... | collective-permute-start | bytes 196616 | tf_op jit(solution)/shard_map/ppermute | solution.py:97
  59.5 0.0 collective-permute-done
  59.5 0.8 collective-permute-done.1
  60.3 0.3 collective-permute-done.2
  60.7 0.1 all_to_all.12
  60.8 23.3 %all_to_all.17 = f32[128,1,256]{2,1,0:T(1,128)S(1)} all-to-all(f32[128,1,256]{2,1,0:T(1,128)S(1)} %all_to_all.12), channel_id=1, replica_groups=mesh['seq'=128,'batch'=4] {'seq'}, dimensions={0} | all-to-all | bytes 262144 | tf_op jit(solution)/shard_map/all_to_all | solution.py:111
  84.2 0.6 slice.214
  84.8 0.6 fusion.19
  (14 shorter events, 0.4 us)
Async XLA Ops:
  0.6 45.8 %copy-start = (f32[896,512]{1,0:T(8,128)S(1)}, f32[896,512]{1,0:T(8,128)}, u32[]{:S(2)}) copy-start(f32[896,512]{1,0:T(8,128)} %constant.16.clone) | copy-start | bytes 5505028
  3.2 42.6 %all-to-all-start = ((f32[128,1,384]{2,1,0:T(1,128)}), f32[128,1,384]{2,1,0:T(1,128)S(1)}, u32[]{:S(2)}, u32[]{:S(2)}) async-start(f32[128,1,384]{2,1,0:T(1,128)} %reshape.18), calls=%async_computation | async-start | bytes 393216 | tf_op jit(solution)/shard_map/all_to_all | solution.py:51
  49.0 10.5 %collective-permute-start = (f32[64,256]{1,0:T(8,128)S(1)}, f32[64,256]{1,0:T(8,128)S(1)}, u32[]{:S(2)}, u32[]{:S(2)}) collective-permute-start(f32[64,256]{1,0:T(8,128)S(1)} %get-tuple-element.5), channel_id=1, source_target_pairs={{0,3},{1,2},{2,1},{3,0},{4,7},{5,6},{6,5},{7,4},{8,11},{9,10},{10,... | collective-permute-start | bytes 196616 | tf_op jit(solution)/shard_map/ppermute | solution.py:97
  54.5 5.8 %collective-permute-start.1 = (f32[64,256]{1,0:T(8,128)S(1)}, f32[64,256]{1,0:T(8,128)S(1)}, u32[]{:S(2)}, u32[]{:S(2)}) collective-permute-start(f32[64,256]{1,0:T(8,128)S(1)} %get-tuple-element.5), channel_id=1, source_target_pairs={{0,2},{1,3},{2,0},{3,1},{4,6},{5,7},{6,4},{7,5},{8,10},{9,11},{10,... | collective-permute-start | bytes 196616 | tf_op jit(solution)/shard_map/ppermute | solution.py:97
  57.5 3.1 %collective-permute-start.2 = (f32[64,256]{1,0:T(8,128)S(1)}, f32[64,256]{1,0:T(8,128)S(1)}, u32[]{:S(2)}, u32[]{:S(2)}) collective-permute-start(f32[64,256]{1,0:T(8,128)S(1)} %get-tuple-element.5), channel_id=1, source_target_pairs={{0,1},{1,0},{2,3},{3,2},{4,5},{5,4},{6,7},{7,6},{8,9},{9,8},{10,11... | collective-permute-start | bytes 196616 | tf_op jit(solution)/shard_map/ppermute | solution.py:97

commit v11 on v10

--- a/solution.py
+++ b/solution.py
@@ -54,56 +54,58 @@
     cotangent = recv[:, 1].reshape(used, inner)
     filt = recv[:, 2].reshape(used, inner)
 
-    stage = contract(first, jnp.concatenate([signal, cotangent, filt], axis=1))
+    partner = lax.ppermute(
+        jnp.stack([signal, cotangent]), "batch", [(i, i ^ 1) for i in range(batch_count)]
+    )
+    odd = (mine & 1) == 1
+    sig_lo = jnp.where(odd, partner[0], signal)
+    cot_lo = jnp.where(odd, partner[1], cotangent)
+    sig_hi = jnp.where(odd, signal, partner[0])
+    cot_hi = jnp.where(odd, cotangent, partner[1])
+    rows = [sig_lo, cot_lo, sig_hi, cot_hi, filt]
+
+    stage = contract(first, jnp.concatenate(rows, axis=1))
     cos_part, sin_part = stage[:outer], stage[outer:]
 
     def twist(re, im, orient):
         return re * tw_cos - orient * im * tw_sin, im * tw_cos + orient * re * tw_sin
 
     parts = []
-    for index in range(3):
+    for index in range(len(rows)):
         cut = slice(index * inner, (index + 1) * inner)
         parts.extend(twist(cos_part[:, cut], -sin_part[:, cut], -1.0))
 
     stage = contract(jnp.concatenate(parts, axis=0), second)
     c2, s2 = stage[:, :inner], stage[:, inner:]
     spectra = []
-    for index in range(3):
+    for index in range(len(rows)):
         re_rows = slice(2 * index * outer, (2 * index + 1) * outer)
         im_rows = slice((2 * index + 1) * outer, (2 * index + 2) * outer)
         spectra.append((c2[re_rows] + s2[im_rows], c2[im_rows] - s2[re_rows]))
-    (xr, xi), (dr, di), (hr, hi) = spectra
+    (xlr, xli), (dlr, dli), (xhr, xhi), (dhr, dhi), (hr, hi) = spectra
+    dr = jnp.where(odd, dhr, dlr)
+    di = jnp.where(odd, dhi, dli)
 
     gx_re = hr * dr + hi * di
     gx_im = hr * di - hi * dr
-    gh_re = xr * dr + xi * di
-    gh_im = xr * di - xi * dr
-    q_re = gx_re - gh_im
-    q_im = gx_im + gh_re
+    gh_re = (xlr * dlr + xli * dli) + (xhr * dhr + xhi * dhi)
+    gh_im = (xlr * dli - xli * dlr) + (xhr * dhi - xhi * dhr)
 
-    stage = contract(jnp.concatenate([q_re, q_im], axis=0), second)
+    stage = contract(jnp.concatenate([gx_re, gx_im, gh_re, gh_im], axis=0), second)
     c2, s2 = stage[:, :inner], stage[:, inner:]
-    g_re = c2[:outer] - s2[outer:]
-    g_im = c2[outer:] + s2[:outer]
-    g_re, g_im = twist(g_re, g_im, 1.0)
-    stage = contract(back, jnp.concatenate([g_re, g_im], axis=1))
+    grads = []
+    for index in range(2):
+        re_rows = slice(2 * index * outer, (2 * index + 1) * outer)
+        im_rows = slice((2 * index + 1) * outer, (2 * index + 2) * outer)
+        grads.extend(twist(c2[re_rows] - s2[im_rows], c2[im_rows] + s2[re_rows], 1.0))
+    stage = contract(back, jnp.concatenate(grads, axis=1))
     c1, s1 = stage[:used], stage[used:]
-    in_row = c1[:, :inner] - s1[:, inner:]
-    filt_row = c1[:, inner:] + s1[:, :inner]
+    in_row = c1[:, :inner] - s1[:, inner : 2 * inner]
+    filt_row = c1[:, 2 * inner : 3 * inner] - s1[:, 3 * inner :]
 
-    received = [filt_row] + [None] * (batch_count - 1)
-    for step in reversed(range(1, batch_count)):
-        pairs = [(index, index ^ step) for index in range(batch_count)]
-        received[step] = lax.ppermute(filt_row, "batch", pairs)
-    ordered = []
-    for source in range(batch_count):
-        pick = received[0]
-        for step in range(1, batch_count):
-            pick = jnp.where((mine ^ step) == source, received[step], pick)
-        ordered.append(pick)
-    filt_row = ordered[0]
-    for source in range(1, batch_count):
-        filt_row = filt_row + ordered[source]
+    filt_row = filt_row + lax.ppermute(
+        filt_row, "batch", [(i, i ^ 2) for i in range(batch_count)]
+    )
 
     send = jnp.concatenate(
         [in_row.reshape(seq_count, length_dev), filt_row.reshape(seq_count, length_dev)], axis=1

time: 86 us -> 85.9 us (level)
  blocking collectives: 23.3 us -> 64.7 us
  starting transfers between devices: 33.4 us -> 7.83 us
  waiting for transfers between devices: 20.8 us -> 3.46 us
  matrix products: 1.9 us -> 2.83 us
    all_to_all x1 -> x2, blocking collectives: 23.3 us -> 64.7 us  [body(): recv = lax.all_to_all(send, 'seq', 0, 0, tiled=True)]
    all_to_all x1 -> x0, starting transfers between devices: 23 us -> none  [body(): recv = lax.all_to_all(send, 'seq', 0, 0, tiled=True)]
    all_to_all x1 -> x0, waiting for transfers between devices: 19.7 us -> none  [body(): recv = lax.all_to_all(send, 'seq', 0, 0, tiled=True)]
    ppermute x3 -> x2, starting transfers between devices: 10.4 us -> 7.83 us  [the longest x1 5.53 us: body(): lax.ppermute(jnp.stack([signal, cotangent]), 'batch', [(i, i ^ 1) for i i...]
    ppermute x3 -> x2, waiting for transfers between devices: 1.17 us -> 3.46 us  [the longest x1 2.68 us: body(): lax.ppermute(filt_row, 'batch', [(i, i ^ 2) for i in range(batch_count)])]
    dot_general x4, matrix products: 1.9 us -> 2.83 us  [contract(): jnp.matmul(left, right, precision=lax.Precision.HIGH, preferred_element_t...]
  transfers between devices with their start and end apart: 4 -> 2, of which waited for: 3 -> 2; matrix products, arithmetic and copies ran while one was open for 0% -> 0% of each run, Pallas kernels for 0% -> 0%
where the time goes in v11:
time: 85.9 us; the launch traced here: 84.6 us
  blocking collectives  64.7 us (75%)
  starting transfers between devices  7.83 us (9%)
  waiting for transfers between devices  3.46 us (4%)
  matrix products  2.83 us (3%)
  other arithmetic  2.74 us (3%)
  local copies, waits for them, and re-layouts  2.06 us (2%)
  between operations  0.94 us (1%)
    all_to_all x2, blocking collectives, body(): recv = lax.all_to_all(send, 'seq', 0, 0, tiled=True)  64.7 us
    ppermute x1, starting transfers between devices, body(): lax.ppermute(jnp.stack([signal, cotangent]), 'batch', [(i, i ^ 1) for i i...  5.53 us
    dot_general x4, matrix products, contract(): jnp.matmul(left, right, precision=lax.Precision.HIGH, preferred_element_t...  2.83 us
    ppermute x1, waiting for transfers between devices, body(): lax.ppermute(filt_row, 'batch', [(i, i ^ 2) for i in range(batch_count)])  2.68 us
    ppermute x1, starting transfers between devices, body(): lax.ppermute(filt_row, 'batch', [(i, i ^ 2) for i in range(batch_count)])  2.31 us
  transfers between devices with their start and end apart: 2, of which 2 were waited for; matrix products, arithmetic and copies ran while one was open for 0% of the time, Pallas kernels for 0%

profile of v11, /device:TPU:1, one launch (start us, length us, event | category | flops | bytes accessed | tf_op | source)
XLA Modules:
  0.0 84.6 jit_solution(6765573576666395807)
XLA Ops:
  0.6 0.8 maximum_convert_fusion
  1.4 0.9 %pad_maximum_fusion = f32[128,384]{1,0:T(8,128)S(1)} fusion(f32[128,128]{1,0:T(8,128)} %param.6, f32[128,256]{1,0:T(8,128)S(1)} %maximum_convert_fusion), kind=kLoop, calls=%fused_computation.19 | loop fusion | flops 49152 | bytes 393216 | tf_op jit(solution)/shard_map/concatenate | solution.py:50
  2.3 0.1 reshape.18
  2.4 42.3 %all_to_all.17 = f32[128,1,384]{2,1,0:T(1,128)S(1)} all-to-all(f32[128,1,384]{2,1,0:T(1,128)S(1)} %reshape.18), channel_id=1, replica_groups=mesh['seq'=128,'batch'=4] {'seq'}, dimensions={0} | all-to-all | bytes 393216 | tf_op jit(solution)/shard_map/all_to_all | solution.py:51
  44.7 0.2 copy.41
  44.9 0.0 copy-start
  44.9 0.1 copy.43
  45.0 0.1 copy.42
  45.2 5.5 %collective-permute-start = (f32[2,64,256]{2,1,0:T(8,128)S(1)}, f32[2,64,256]{2,1,0:T(8,128)S(1)}, u32[]{:S(2)}, u32[]{:S(2)}) collective-permute-start(f32[2,64,256]{2,1,0:T(8,128)S(1)} %pad_maximum_fusion.1), channel_id=1, source_target_pairs={{0,1},{1,0},{2,3},{3,2},{4,5},{5,4},{6,7},{7,6},{8,9},{9,8},{10,11... | collective-permute-start | bytes 393224 | tf_op jit(solution)/shard_map/ppermute | solution.py:57
  50.8 0.1 copy.46
  50.9 0.8 collective-permute-done
  51.8 0.0 copy-done
  51.8 0.7 fusion.19
  52.5 0.1 subtract_dynamic-update-slice_fusion.3
  52.6 0.1 add_dynamic-update-slice_fusion.3
  52.7 0.1 subtract_dynamic-update-slice_fusion.1
  52.8 0.1 add_dynamic-update-slice_fusion.1
  53.0 1.2 %fusion.17 = f32[1280,512]{1,0:T(8,128)S(1)} fusion(f32[1280,256]{1,0:T(8,128)S(1)} %add_dynamic-update-slice_fusion, f32[896,512]{1,0:T(8,128)S(1)} %copy-done), kind=kOutput, calls=%fused_computation.17 | convolution fusion | flops 1006632960 | bytes 4456448 | tf_op jit(solution)/shard_map/dot_general | solution.py:10
  54.2 0.1 multiply_add_fusion.2
  54.3 0.1 add_add_fusion
  54.4 0.1 multiply_subtract_fusion.2
  54.5 0.6 fusion
  55.1 0.1 multiply_add_fusion
  55.2 0.1 multiply_subtract_fusion.1
  55.3 0.4 fusion.8
  55.7 2.3 %collective-permute-start.1 = (f32[64,256]{1,0:T(8,128)S(1)}, f32[64,256]{1,0:T(8,128)S(1)}, u32[]{:S(2)}, u32[]{:S(2)}) collective-permute-start(f32[64,256]{1,0:T(8,128)S(1)} %get-tuple-element.13), channel_id=1, source_target_pairs={{0,2},{1,3},{2,0},{3,1},{4,6},{5,7},{6,4},{7,5},{8,10},{9,11},{10,... | collective-permute-start | bytes 196616 | tf_op jit(solution)/shard_map/ppermute | solution.py:106
  58.0 2.7 %collective-permute-done.1 = f32[64,256]{1,0:T(8,128)S(1)} collective-permute-done((f32[64,256]{1,0:T(8,128)S(1)}, f32[64,256]{1,0:T(8,128)S(1)}, u32[]{:S(2)}, u32[]{:S(2)}) %collective-permute-start.1) | collective-permute-done | bytes 65568 | tf_op jit(solution)/shard_map/ppermute | solution.py:106
  60.8 0.1 all_to_all.12
  60.9 22.4 %all_to_all.18 = f32[128,1,256]{2,1,0:T(1,128)S(1)} all-to-all(f32[128,1,256]{2,1,0:T(1,128)S(1)} %all_to_all.12), channel_id=1, replica_groups=mesh['seq'=128,'batch'=4] {'seq'}, dimensions={0} | all-to-all | bytes 262144 | tf_op jit(solution)/shard_map/all_to_all | solution.py:113
  83.3 0.6 fusion.22
  83.9 0.6 slice.322
  (24 shorter events, 0.5 us)
Async XLA Ops:
  44.9 6.9 %copy-start = (f32[896,512]{1,0:T(8,128)S(1)}, f32[896,512]{1,0:T(8,128)}, u32[]{:S(2)}) copy-start(f32[896,512]{1,0:T(8,128)} %constant.10.clone) | copy-start | bytes 5505028
  45.2 6.5 %collective-permute-start = (f32[2,64,256]{2,1,0:T(8,128)S(1)}, f32[2,64,256]{2,1,0:T(8,128)S(1)}, u32[]{:S(2)}, u32[]{:S(2)}) collective-permute-start(f32[2,64,256]{2,1,0:T(8,128)S(1)} %pad_maximum_fusion.1), channel_id=1, source_target_pairs={{0,1},{1,0},{2,3},{3,2},{4,5},{5,4},{6,7},{7,6},{8,9},{9,8},{10,11... | collective-permute-start | bytes 393224 | tf_op jit(solution)/shard_map/ppermute | solution.py:57
  55.7 5.0 %collective-permute-start.1 = (f32[64,256]{1,0:T(8,128)S(1)}, f32[64,256]{1,0:T(8,128)S(1)}, u32[]{:S(2)}, u32[]{:S(2)}) collective-permute-start(f32[64,256]{1,0:T(8,128)S(1)} %get-tuple-element.13), channel_id=1, source_target_pairs={{0,2},{1,3},{2,0},{3,1},{4,6},{5,7},{6,4},{7,5},{8,10},{9,11},{10,... | collective-permute-start | bytes 196616 | tf_op jit(solution)/shard_map/ppermute | solution.py:106

commit v12 on v11

--- a/solution.py
+++ b/solution.py
@@ -91,21 +91,18 @@
     gh_re = (xlr * dlr + xli * dli) + (xhr * dhr + xhi * dhi)
     gh_im = (xlr * dli - xli * dlr) + (xhr * dhi - xhi * dhr)
 
-    stage = contract(jnp.concatenate([gx_re, gx_im, gh_re, gh_im], axis=0), second)
-    c2, s2 = stage[:, :inner], stage[:, inner:]
-    grads = []
-    for index in range(2):
-        re_rows = slice(2 * index * outer, (2 * index + 1) * outer)
-        im_rows = slice((2 * index + 1) * outer, (2 * index + 2) * outer)
-        grads.extend(twist(c2[re_rows] - s2[im_rows], c2[im_rows] + s2[re_rows], 1.0))
-    stage = contract(back, jnp.concatenate(grads, axis=1))
-    c1, s1 = stage[:used], stage[used:]
-    in_row = c1[:, :inner] - s1[:, inner : 2 * inner]
-    filt_row = c1[:, 2 * inner : 3 * inner] - s1[:, 3 * inner :]
+    def inverse(re, im):
+        stage = contract(jnp.concatenate([re, im], axis=0), second)
+        c2, s2 = stage[:, :inner], stage[:, inner:]
+        g_re, g_im = twist(c2[:outer] - s2[outer:], c2[outer:] + s2[:outer], 1.0)
+        stage = contract(back, jnp.concatenate([g_re, g_im], axis=1))
+        return stage[:used, :inner] - stage[used:, inner:]
 
-    filt_row = filt_row + lax.ppermute(
-        filt_row, "batch", [(i, i ^ 2) for i in range(batch_count)]
-    )
+    filt_row = inverse(gh_re, gh_im)
+    filt_row, gx_re, gx_im = lax.optimization_barrier((filt_row, gx_re, gx_im))
+    other = lax.ppermute(filt_row, "batch", [(i, i ^ 2) for i in range(batch_count)])
+    in_row = inverse(gx_re, gx_im)
+    filt_row = filt_row + other
 
     send = jnp.concatenate(
         [in_row.reshape(seq_count, length_dev), filt_row.reshape(seq_count, length_dev)], axis=1

time: 85.9 us -> 85.4 us (level)
    dot_general x4 -> x6, matrix products: 2.83 us -> 3.13 us  [contract(): jnp.matmul(left, right, precision=lax.Precision.HIGH, preferred_element_t...]
  transfers between devices with their start and end apart: 2 -> 2, of which waited for: 2 -> 2; matrix products, arithmetic and copies ran while one was open for 0% -> 1% of each run, Pallas kernels for 0% -> 0%
where the time goes in v12:
time: 85.4 us; the launch traced here: 84.1 us
  blocking collectives  64.7 us (76%)
  starting transfers between devices  7.83 us (9%)
  matrix products  3.13 us (4%)
  other arithmetic  2.72 us (3%)
  waiting for transfers between devices  2.71 us (3%)
  local copies, waits for them, and re-layouts  2.06 us (2%)
  between operations  0.95 us (1%)
    all_to_all x2, blocking collectives, body(): recv = lax.all_to_all(send, 'seq', 0, 0, tiled=True)  64.7 us
    ppermute x1, starting transfers between devices, body(): lax.ppermute(jnp.stack([signal, cotangent]), 'batch', [(i, i ^ 1) for i i...  5.53 us
    dot_general x6, matrix products, contract(): jnp.matmul(left, right, precision=lax.Precision.HIGH, preferred_element_t...  3.13 us
    ppermute x1, starting transfers between devices, body(): lax.ppermute(filt_row, 'batch', [(i, i ^ 2) for i in range(batch_count)])  2.31 us
    ppermute x1, waiting for transfers between devices, body(): lax.ppermute(filt_row, 'batch', [(i, i ^ 2) for i in range(batch_count)])  1.93 us
  transfers between devices with their start and end apart: 2, of which 2 were waited for; matrix products, arithmetic and copies ran while one was open for 1% of the time, Pallas kernels for 0%

profile of v12, /device:TPU:1, one launch (start us, length us, event | category | flops | bytes accessed | tf_op | source)
XLA Modules:
  0.0 84.1 jit_solution(6464891811950319620)
XLA Ops:
  0.6 0.8 maximum_convert_fusion
  1.4 0.9 %pad_maximum_fusion = f32[128,384]{1,0:T(8,128)S(1)} fusion(f32[128,128]{1,0:T(8,128)} %param.6, f32[128,256]{1,0:T(8,128)S(1)} %maximum_convert_fusion), kind=kLoop, calls=%fused_computation.20 | loop fusion | flops 49152 | bytes 393216 | tf_op jit(solution)/shard_map/concatenate | solution.py:50
  2.3 0.1 reshape.18
  2.4 42.3 %all_to_all.17 = f32[128,1,384]{2,1,0:T(1,128)S(1)} all-to-all(f32[128,1,384]{2,1,0:T(1,128)S(1)} %reshape.18), channel_id=1, replica_groups=mesh['seq'=128,'batch'=4] {'seq'}, dimensions={0} | all-to-all | bytes 393216 | tf_op jit(solution)/shard_map/all_to_all | solution.py:51
  44.7 0.2 copy.17
  44.9 0.0 copy-start
  44.9 0.1 copy.19
  45.0 0.1 copy.18
  45.2 5.5 %collective-permute-start = (f32[2,64,256]{2,1,0:T(8,128)S(1)}, f32[2,64,256]{2,1,0:T(8,128)S(1)}, u32[]{:S(2)}, u32[]{:S(2)}) collective-permute-start(f32[2,64,256]{2,1,0:T(8,128)S(1)} %pad_maximum_fusion.1), channel_id=1, source_target_pairs={{0,1},{1,0},{2,3},{3,2},{4,5},{5,4},{6,7},{7,6},{8,9},{9,8},{10,11... | collective-permute-start | bytes 393224 | tf_op jit(solution)/shard_map/ppermute | solution.py:57
  50.8 0.1 copy.22
  50.9 0.8 collective-permute-done
  51.8 0.0 copy-done
  51.8 0.7 fusion.20
  52.5 0.1 subtract_dynamic-update-slice_fusion.3
  52.6 0.1 add_dynamic-update-slice_fusion.3
  52.7 0.1 subtract_dynamic-update-slice_fusion.1
  52.8 0.1 add_dynamic-update-slice_fusion.1
  53.0 1.2 %fusion.4 = f32[1280,512]{1,0:T(8,128)S(1)} fusion(f32[1280,256]{1,0:T(8,128)S(1)} %add_dynamic-update-slice_fusion, f32[896,512]{1,0:T(8,128)S(1)} %copy-done), kind=kOutput, calls=%fused_computation.4 | convolution fusion | flops 1006632960 | bytes 4456448 | tf_op jit(solution)/shard_map/dot_general | solution.py:10
  54.2 0.1 multiply_subtract_fusion.1
  54.3 0.1 add_add_fusion
  54.4 0.1 multiply_add_fusion.1
  54.5 0.4 fusion.2
  54.9 0.1 multiply_subtract_fusion.2
  55.0 0.3 fusion.9
  55.3 2.3 %collective-permute-start.1 = (f32[64,256]{1,0:T(8,128)S(1)}, f32[64,256]{1,0:T(8,128)S(1)}, u32[]{:S(2)}, u32[]{:S(2)}) collective-permute-start(f32[64,256]{1,0:T(8,128)S(1)} %slice_subtract_fusion.8), channel_id=1, source_target_pairs={{0,2},{1,3},{2,0},{3,1},{4,6},{5,7},{6,4},{7,5},{8,10},{9,11},{10,... | collective-permute-start | bytes 196616 | tf_op jit(solution)/shard_map/ppermute | solution.py:103
  57.6 0.4 fusion
  58.0 0.1 multiply_subtract_fusion
  58.1 0.3 fusion.16
  58.4 1.9 %collective-permute-done.1 = f32[64,256]{1,0:T(8,128)S(1)} collective-permute-done((f32[64,256]{1,0:T(8,128)S(1)}, f32[64,256]{1,0:T(8,128)S(1)}, u32[]{:S(2)}, u32[]{:S(2)}) %collective-permute-start.1) | collective-permute-done | bytes 65568 | tf_op jit(solution)/shard_map/ppermute | solution.py:103
  60.3 0.1 all_to_all.12
  60.4 22.4 %all_to_all.18 = f32[128,1,256]{2,1,0:T(1,128)S(1)} all-to-all(f32[128,1,256]{2,1,0:T(1,128)S(1)} %all_to_all.12), channel_id=1, replica_groups=mesh['seq'=128,'batch'=4] {'seq'}, dimensions={0} | all-to-all | bytes 262144 | tf_op jit(solution)/shard_map/all_to_all | solution.py:110
  82.9 0.6 fusion.24
  83.5 0.6 slice.318
  (25 shorter events, 0.5 us)
Async XLA Ops:
  44.9 6.9 %copy-start = (f32[896,512]{1,0:T(8,128)S(1)}, f32[896,512]{1,0:T(8,128)}, u32[]{:S(2)}) copy-start(f32[896,512]{1,0:T(8,128)} %constant.10.clone) | copy-start | bytes 5505028
  45.2 6.5 %collective-permute-start = (f32[2,64,256]{2,1,0:T(8,128)S(1)}, f32[2,64,256]{2,1,0:T(8,128)S(1)}, u32[]{:S(2)}, u32[]{:S(2)}) collective-permute-start(f32[2,64,256]{2,1,0:T(8,128)S(1)} %pad_maximum_fusion.1), channel_id=1, source_target_pairs={{0,1},{1,0},{2,3},{3,2},{4,5},{5,4},{6,7},{7,6},{8,9},{9,8},{10,11... | collective-permute-start | bytes 393224 | tf_op jit(solution)/shard_map/ppermute | solution.py:57
  55.3 5.0 %collective-permute-start.1 = (f32[64,256]{1,0:T(8,128)S(1)}, f32[64,256]{1,0:T(8,128)S(1)}, u32[]{:S(2)}, u32[]{:S(2)}) collective-permute-start(f32[64,256]{1,0:T(8,128)S(1)} %slice_subtract_fusion.8), channel_id=1, source_target_pairs={{0,2},{1,3},{2,0},{3,1},{4,6},{5,7},{6,4},{7,5},{8,10},{9,11},{10,... | collective-permute-start | bytes 196616 | tf_op jit(solution)/shard_map/ppermute | solution.py:103

commit v13 on v12

--- a/solution.py
+++ b/solution.py
@@ -58,33 +58,33 @@
         jnp.stack([signal, cotangent]), "batch", [(i, i ^ 1) for i in range(batch_count)]
     )
     odd = (mine & 1) == 1
-    sig_lo = jnp.where(odd, partner[0], signal)
-    cot_lo = jnp.where(odd, partner[1], cotangent)
-    sig_hi = jnp.where(odd, signal, partner[0])
-    cot_hi = jnp.where(odd, cotangent, partner[1])
-    rows = [sig_lo, cot_lo, sig_hi, cot_hi, filt]
-
-    stage = contract(first, jnp.concatenate(rows, axis=1))
-    cos_part, sin_part = stage[:outer], stage[outer:]
 
     def twist(re, im, orient):
         return re * tw_cos - orient * im * tw_sin, im * tw_cos + orient * re * tw_sin
 
-    parts = []
-    for index in range(len(rows)):
-        cut = slice(index * inner, (index + 1) * inner)
-        parts.extend(twist(cos_part[:, cut], -sin_part[:, cut], -1.0))
+    def forward(rows):
+        stage = contract(first, jnp.concatenate(rows, axis=1))
+        cos_part, sin_part = stage[:outer], stage[outer:]
+        parts = []
+        for index in range(len(rows)):
+            cut = slice(index * inner, (index + 1) * inner)
+            parts.extend(twist(cos_part[:, cut], -sin_part[:, cut], -1.0))
+        stage = contract(jnp.concatenate(parts, axis=0), second)
+        c2, s2 = stage[:, :inner], stage[:, inner:]
+        spectra = []
+        for index in range(len(rows)):
+            re_rows = slice(2 * index * outer, (2 * index + 1) * outer)
+            im_rows = slice((2 * index + 1) * outer, (2 * index + 2) * outer)
+            spectra.append((c2[re_rows] + s2[im_rows], c2[im_rows] - s2[re_rows]))
+        return spectra
 
-    stage = contract(jnp.concatenate(parts, axis=0), second)
-    c2, s2 = stage[:, :inner], stage[:, inner:]
-    spectra = []
-    for index in range(len(rows)):
-        re_rows = slice(2 * index * outer, (2 * index + 1) * outer)
-        im_rows = slice((2 * index + 1) * outer, (2 * index + 2) * outer)
-        spectra.append((c2[re_rows] + s2[im_rows], c2[im_rows] - s2[re_rows]))
-    (xlr, xli), (dlr, dli), (xhr, xhi), (dhr, dhi), (hr, hi) = spectra
-    dr = jnp.where(odd, dhr, dlr)
-    di = jnp.where(odd, dhi, dli)
+    own = forward([signal, cotangent, filt])
+    other = forward([partner[0], partner[1], filt])
+    pick = lambda a, b: tuple(jnp.where(odd, v, u) for u, v in zip(a, b))
+    (xlr, xli), (dlr, dli) = pick(own[0], other[0]), pick(own[1], other[1])
+    (xhr, xhi), (dhr, dhi) = pick(other[0], own[0]), pick(other[1], own[1])
+    hr, hi = own[2]
+    dr, di = own[1]
 
     gx_re = hr * dr + hi * di
     gx_im = hr * di - hi * dr

time: 85.4 us -> 86.6 us (1.014)
  blocking collectives: 64.7 us -> 22.4 us
  starting transfers between devices: 7.83 us -> 30.5 us
  waiting for transfers between devices: 2.71 us -> 22.1 us
    all_to_all x2 -> x1, blocking collectives: 64.7 us -> 22.4 us  [body(): recv = lax.all_to_all(send, 'seq', 0, 0, tiled=True)]
    all_to_all x0 -> x1, starting transfers between devices: none -> 23 us  [body(): recv = lax.all_to_all(send, 'seq', 0, 0, tiled=True)]
    all_to_all x0 -> x1, waiting for transfers between devices: none -> 19.7 us  [body(): recv = lax.all_to_all(send, 'seq', 0, 0, tiled=True)]
    dot_general x6 -> x8, matrix products: 3.13 us -> 3.8 us  [contract(): jnp.matmul(left, right, precision=lax.Precision.HIGH, preferred_element_t...]
  transfers between devices with their start and end apart: 2 -> 3, of which waited for: 2 -> 3; matrix products, arithmetic and copies ran while one was open for 1% -> 1% of each run, Pallas kernels for 0% -> 0%
where the time goes in v13:
time: 86.6 us; the launch traced here: 85.4 us
  starting transfers between devices  30.5 us (35%)
  blocking collectives  22.4 us (26%)
  waiting for transfers between devices  22.1 us (26%)
  matrix products  3.8 us (4%)
  other arithmetic  2.85 us (3%)
  local copies, waits for them, and re-layouts  2.74 us (3%)
  between operations  0.96 us (1%)
    all_to_all x1, starting transfers between devices, body(): recv = lax.all_to_all(send, 'seq', 0, 0, tiled=True)  23 us
    all_to_all x1, blocking collectives, body(): recv = lax.all_to_all(send, 'seq', 0, 0, tiled=True)  22.4 us
    all_to_all x1, waiting for transfers between devices, body(): recv = lax.all_to_all(send, 'seq', 0, 0, tiled=True)  19.7 us
    ppermute x1, starting transfers between devices, body(): lax.ppermute(jnp.stack([signal, cotangent]), 'batch', [(i, i ^ 1) for i i...  5.24 us
    dot_general x8, matrix products, contract(): jnp.matmul(left, right, precision=lax.Precision.HIGH, preferred_element_t...  3.8 us
    ppermute x1, starting transfers between devices, body(): lax.ppermute(filt_row, 'batch', [(i, i ^ 2) for i in range(batch_count)])  2.31 us
    ppermute x1, waiting for transfers between devices, body(): lax.ppermute(filt_row, 'batch', [(i, i ^ 2) for i in range(batch_count)])  1.93 us
  transfers between devices with their start and end apart: 3, of which 3 were waited for; matrix products, arithmetic and copies ran while one was open for 1% of the time, Pallas kernels for 0%

profile of v13, /device:TPU:1, one launch (start us, length us, event | category | flops | bytes accessed | tf_op | source)
XLA Modules:
  0.0 85.4 jit_solution(10440970131364858269)
XLA Ops:
  0.6 0.0 copy-start
  0.6 0.9 %maximum_convert_fusion = f32[128,256]{1,0:T(8,128)S(1)} fusion(bf16[128,128]{1,0:T(8,128)(2,1)} %bitcast.27, bf16[128,128]{1,0:T(8,128)(2,1)} %bitcast.28), kind=kLoop, calls=%fused_computation.83 | loop fusion | flops 131072 | bytes 196608 | tf_op jit(solution)/shard_map/convert_element_type | solution.py:49
  1.6 0.9 %pad_maximum_fusion.4 = f32[128,384]{1,0:T(8,128)S(1)} fusion(f32[128,128]{1,0:T(8,128)} %param.6, f32[128,256]{1,0:T(8,128)S(1)} %maximum_convert_fusion), kind=kLoop, calls=%fused_computation.26 | loop fusion | flops 49152 | bytes 393216 | tf_op jit(solution)/shard_map/concatenate | solution.py:50
  2.4 0.8 reshape.18
  3.2 23.0 %all-to-all-start = ((f32[128,1,384]{2,1,0:T(1,128)}), f32[128,1,384]{2,1,0:T(1,128)S(1)}, u32[]{:S(2)}, u32[]{:S(2)}) async-start(f32[128,1,384]{2,1,0:T(1,128)} %reshape.18), calls=%async_computation | async-start | bytes 393216 | tf_op jit(solution)/shard_map/all_to_all | solution.py:51
  26.2 19.7 %all-to-all-done = f32[128,1,384]{2,1,0:T(1,128)S(1)} async-done(((f32[128,1,384]{2,1,0:T(1,128)}), f32[128,1,384]{2,1,0:T(1,128)S(1)}, u32[]{:S(2)}, u32[]{:S(2)}) %all-to-all-start) | async-done | bytes 196640 | tf_op jit(solution)/shard_map/all_to_all | solution.py:51
  45.9 0.2 copy.17
  46.1 0.1 copy.19
  46.2 0.1 copy.18
  46.4 0.1 copy.20
  46.5 5.2 %collective-permute-start = (f32[2,64,256]{2,1,0:T(8,128)S(1)}, f32[2,64,256]{2,1,0:T(8,128)S(1)}, u32[]{:S(2)}, u32[]{:S(2)}) collective-permute-start(f32[2,64,256]{2,1,0:T(8,128)S(1)} %pad_maximum_fusion.5), channel_id=1, source_target_pairs={{0,1},{1,0},{2,3},{3,2},{4,5},{5,4},{6,7},{7,6},{8,9},{9,8},{10,11... | collective-permute-start | bytes 393224 | tf_op jit(solution)/shard_map/ppermute | solution.py:57
  51.8 0.0 copy-done
  51.8 0.5 fusion.23
  52.2 0.5 collective-permute-done
  52.7 0.5 fusion.22
  53.3 0.1 subtract_dynamic-update-slice_fusion.4
  53.4 0.1 add_dynamic-update-slice_fusion.4
  53.5 0.1 add_dynamic-update-slice_fusion.3
  53.5 0.8 fusion.6
  54.6 0.8 fusion.4
  55.4 0.1 multiply_subtract_fusion.1
  55.5 0.1 add_add_fusion
  55.6 0.2 multiply_add_fusion.1
  55.8 0.4 fusion.2
  56.2 0.1 multiply_subtract_fusion.2
  56.2 0.3 fusion.11
  56.5 2.3 %collective-permute-start.1 = (f32[64,256]{1,0:T(8,128)S(1)}, f32[64,256]{1,0:T(8,128)S(1)}, u32[]{:S(2)}, u32[]{:S(2)}) collective-permute-start(f32[64,256]{1,0:T(8,128)S(1)} %slice_subtract_fusion.8), channel_id=1, source_target_pairs={{0,2},{1,3},{2,0},{3,1},{4,6},{5,7},{6,4},{7,5},{8,10},{9,11},{10,... | collective-permute-start | bytes 196616 | tf_op jit(solution)/shard_map/ppermute | solution.py:103
  58.8 0.4 fusion
  59.2 0.1 multiply_subtract_fusion
  59.3 0.3 fusion.18
  59.6 1.9 %collective-permute-done.1 = f32[64,256]{1,0:T(8,128)S(1)} collective-permute-done((f32[64,256]{1,0:T(8,128)S(1)}, f32[64,256]{1,0:T(8,128)S(1)}, u32[]{:S(2)}, u32[]{:S(2)}) %collective-permute-start.1) | collective-permute-done | bytes 65568 | tf_op jit(solution)/shard_map/ppermute | solution.py:103
  61.6 0.1 all_to_all.12
  61.7 22.4 %all_to_all.17 = f32[128,1,256]{2,1,0:T(1,128)S(1)} all-to-all(f32[128,1,256]{2,1,0:T(1,128)S(1)} %all_to_all.12), channel_id=1, replica_groups=mesh['seq'=128,'batch'=4] {'seq'}, dimensions={0} | all-to-all | bytes 262144 | tf_op jit(solution)/shard_map/all_to_all | solution.py:110
  84.1 0.6 fusion.34
  84.7 0.6 slice.332
  (23 shorter events, 0.6 us)
Async XLA Ops:
  0.6 51.1 %copy-start = (f32[896,512]{1,0:T(8,128)S(1)}, f32[896,512]{1,0:T(8,128)}, u32[]{:S(2)}) copy-start(f32[896,512]{1,0:T(8,128)} %constant.10.clone) | copy-start | bytes 5505028
  3.2 42.6 %all-to-all-start = ((f32[128,1,384]{2,1,0:T(1,128)}), f32[128,1,384]{2,1,0:T(1,128)S(1)}, u32[]{:S(2)}, u32[]{:S(2)}) async-start(f32[128,1,384]{2,1,0:T(1,128)} %reshape.18), calls=%async_computation | async-start | bytes 393216 | tf_op jit(solution)/shard_map/all_to_all | solution.py:51
  46.5 6.2 %collective-permute-start = (f32[2,64,256]{2,1,0:T(8,128)S(1)}, f32[2,64,256]{2,1,0:T(8,128)S(1)}, u32[]{:S(2)}, u32[]{:S(2)}) collective-permute-start(f32[2,64,256]{2,1,0:T(8,128)S(1)} %pad_maximum_fusion.5), channel_id=1, source_target_pairs={{0,1},{1,0},{2,3},{3,2},{4,5},{5,4},{6,7},{7,6},{8,9},{9,8},{10,11... | collective-permute-start | bytes 393224 | tf_op jit(solution)/shard_map/ppermute | solution.py:57
  56.5 5.0 %collective-permute-start.1 = (f32[64,256]{1,0:T(8,128)S(1)}, f32[64,256]{1,0:T(8,128)S(1)}, u32[]{:S(2)}, u32[]{:S(2)}) collective-permute-start(f32[64,256]{1,0:T(8,128)S(1)} %slice_subtract_fusion.8), channel_id=1, source_target_pairs={{0,2},{1,3},{2,0},{3,1},{4,6},{5,7},{6,4},{7,5},{8,10},{9,11},{10,... | collective-permute-start | bytes 196616 | tf_op jit(solution)/shard_map/ppermute | solution.py:103
